TPU v7x, 512 devices: a whole 4x4x16 slice. The times are simulated.
512 devices in a mesh: rep: 64 (over z, x_lo, core), tile: 8 (over y, x_hi).
Axes of the slice: x: 4 (x_hi: 2, x_lo: 2; x = x_hi * 2 + x_lo), y: 4, z: 16, core: 2. Of those that a mesh axis runs over, the one named last changes fastest.
Arguments:
- images: bfloat16 [2, 64, 1, 16, 256, 128], P(None, 'rep', None, 'tile'), may hold values from -12 to 12
- out_grads: bfloat16 [2, 64, 1, 16, 256, 128], P(None, 'rep', None, 'tile'), may hold values from -12 to 12
- numerators: float32 [64, 2, 1152, 128], P('rep'), may hold values from -5 to 5
- push_weight: float32 [64], P('rep'), may hold values from 0.5 to 2
- step_index: int32 [1], replicated, may hold values from 0 to 999
Outputs:
- new_numerators: float32 [64, 2, 1152, 128], P('rep')
- new_weight: float32 [64], P('rep')
Inputs may be any that keep to these rules, and one draw needn't show every extreme that they name: Step s of the window pairs replica r with replica r - 2 ** ((step_index + s) mod log2 64).
All inputs are finite; a program needn't handle non-finite values.
Results may differ from a plain program's by a relative error of at most 0.01.
Values may be sent and summed in bfloat16 or wider, within the bound.
No kernel may reach another device: no remote copies, remote signals or barrier semaphores. Data moves between devices by JAX's collectives and lax.ppermute only.
A program may use at most 64 MiB of HBM per device.

v0:
```python
from functools import partial
import math

import jax
import jax.numpy as jnp
from jax import lax
from jax.sharding import PartitionSpec as P

learn_rate = 0.03


def passed_along(shard, axis, by):
    devices = lax.axis_size(axis)
    return lax.ppermute(shard, axis, [(i, (i + by) % devices) for i in range(devices)])


def with_halo(shard, sides, width):
    for axis, dim in sides:
        devices, length = (lax.axis_size(axis), shard.shape[dim])
        up = [(i, (i + 1) % devices) for i in range(devices - 1)]
        down = [(j, i) for i, j in up]
        last = lax.slice_in_dim(shard, length - width, length, axis=dim)
        leading = lax.slice_in_dim(shard, 0, width, axis=dim)
        before = lax.ppermute(last, axis, up)
        after = lax.ppermute(leading, axis, down)
        shard = jnp.concatenate([before, shard, after], axis=dim)
    return shard


def pad_columns(field_in):
    return jnp.pad(field_in, ((0, 0), (0, 0), (1, 1), (0, 0)))


def patches(padded):
    out_rows = padded.shape[1] - 2
    out_cols = padded.shape[2] - 2
    pieces = [
        padded[:, row_off : row_off + out_rows, col_off : col_off + out_cols, :]
        for row_off in range(3)
        for col_off in range(3)
    ]
    return jnp.concatenate(pieces, axis=-1).reshape(-1, 9 * padded.shape[3])


def flipped(kernel):
    channels = kernel.shape[1]
    return (
        kernel.reshape(3, 3, channels, channels)[::-1, ::-1]
        .transpose(0, 1, 3, 2)
        .reshape(9 * channels, channels)
    )


def contract_rows(left_mat, right_mat):
    return lax.dot_general(
        left_mat, right_mat, (((0,), (0,)), ((), ())), preferred_element_type=jnp.float32
    )


def push_whole(payload, distance):
    return passed_along(payload, "rep", distance)


def shards(images, out_grads, numerators, push_weight, step_index):
    levels = lax.axis_size("rep").bit_length() - 1
    batch_size = images.shape[2]
    own_rows = images.shape[3]
    columns = images.shape[4]
    channels = images.shape[5]
    norm_scale = 1.0 / math.sqrt(9 * channels)
    sum_state = numerators[0]
    weight = push_weight
    for step_num in range(images.shape[0]):
        weights = (sum_state / weight[0]).astype(jnp.bfloat16)
        grad_own = out_grads[step_num, 0]
        extended = with_halo(images[step_num, 0], (("tile", 1),), 1)
        input_patches = patches(pad_columns(extended))
        pre_act = norm_scale * jnp.dot(
            input_patches, weights[0], preferred_element_type=jnp.float32
        )
        hidden = (
            jax.nn.silu(pre_act)
            .astype(jnp.bfloat16)
            .reshape(batch_size, own_rows, columns, channels)
        )
        hidden_rows = with_halo(hidden, (("tile", 1),), 1)
        grad_rows = with_halo(grad_own, (("tile", 1),), 1)
        hidden_patches = patches(pad_columns(hidden_rows))
        grad_patches = patches(pad_columns(grad_rows))
        grad_hidden = norm_scale * jnp.dot(
            grad_patches, flipped(weights[1]), preferred_element_type=jnp.float32
        )
        sigmoid_val = jax.nn.sigmoid(pre_act)
        grad_pre = (grad_hidden * sigmoid_val * (1.0 + pre_act * (1.0 - sigmoid_val))).astype(
            jnp.bfloat16
        )
        first_grad = norm_scale * contract_rows(input_patches, grad_pre)
        second = norm_scale * contract_rows(hidden_patches, grad_own.reshape(-1, channels))
        local_grads = jnp.stack([first_grad, second])
        peer_level = (step_index[0] + step_num) % levels
        summed = lax.psum(local_grads.astype(jnp.bfloat16), "tile").astype(jnp.float32)
        sum_state = sum_state - learn_rate * summed
        branches = [partial(push_whole, distance=1 << bit_num) for bit_num in range(levels)]
        got_state, got_weight = lax.switch(peer_level, branches, (sum_state, weight))
        sum_state = 0.5 * (sum_state + got_state)
        weight = 0.5 * (weight + got_weight)
    return (sum_state[None], weight)


def solution(mesh):
    in_specs = (
        P(None, "rep", None, "tile", None, None),
        P(None, "rep", None, "tile", None, None),
        P("rep", None, None, None),
        P("rep"),
        P(),
    )
    out_specs = (P("rep", None, None, None), P("rep"))
    return jax.shard_map(shards, mesh=mesh, in_specs=in_specs, out_specs=out_specs, check_vma=False)
```

profile of v0, /device:TPU:96, one launch (start us, length us, event | category | flops | bytes accessed | tf_op | source)
XLA Modules:
  0.0 463.9 jit_solution(18045209188929427469)
XLA Ops:
  7.2 1.1 slice_bitcast_fusion.4
  9.0 5.5 %collective-permute-start.26 = (bf16[1,1,256,128]{3,2,1,0:T(8,128)(2,1)}, bf16[1,1,256,128]{3,2,1,0:T(8,128)(2,1)}, u32[]{:S(2)}, u32[]{:S(2)}) collective-permute-start(bf16[1,1,256,128]{3,2,1,0:T(8,128)(2,1)} %get-tuple-element.136), channel_id=1, source_target_pairs={{0,1},{1,2},{2,3},{3,4},{4,5},{5,6},{6,7},{8,9},{9,10},{10,11},{11... | collective-permute-start | bytes 196616 | tf_op jit(solution)/shard_map/ppermute | solution.py:24
  14.6 1.3 collective-permute-start.27
  16.6 6.0 %collective-permute-start.24 = (bf16[1,1,256,128]{3,2,1,0:T(8,128)(2,1)}, bf16[1,1,256,128]{3,2,1,0:T(8,128)(2,1)S(1)}, u32[]{:S(2)}, u32[]{:S(2)}) collective-permute-start(bf16[1,1,256,128]{3,2,1,0:T(8,128)(2,1)} %get-tuple-element.144), channel_id=1, source_target_pairs={{0,1},{1,2},{2,3},{3,4},{4,5},{5,6},{6,7},{8,9},{9,10},{10,11},{11... | collective-permute-start | bytes 196616 | tf_op jit(solution)/shard_map/ppermute | solution.py:24
  22.7 1.3 collective-permute-start.25
  24.6 6.0 %collective-permute-start.30 = (bf16[1,1,256,128]{3,2,1,0:T(8,128)(2,1)}, bf16[1,1,256,128]{3,2,1,0:T(8,128)(2,1)S(1)}, u32[]{:S(2)}, u32[]{:S(2)}) collective-permute-start(bf16[1,1,256,128]{3,2,1,0:T(8,128)(2,1)} %get-tuple-element.148), channel_id=1, source_target_pairs={{0,1},{1,2},{2,3},{3,4},{4,5},{5,6},{6,7},{8,9},{9,10},{10,11},{11... | collective-permute-start | bytes 196616 | tf_op jit(solution)/shard_map/ppermute | solution.py:24
  33.0 1.3 collective-permute-start.31
  34.4 6.2 %collective-permute-start.32 = (bf16[1,1,256,128]{3,2,1,0:T(8,128)(2,1)}, bf16[1,1,256,128]{3,2,1,0:T(8,128)(2,1)S(1)}, u32[]{:S(2)}, u32[]{:S(2)}) collective-permute-start(bf16[1,1,256,128]{3,2,1,0:T(8,128)(2,1)} %get-tuple-element.128), channel_id=1, source_target_pairs={{0,1},{1,2},{2,3},{3,4},{4,5},{5,6},{6,7},{8,9},{9,10},{10,11},{11... | collective-permute-start | bytes 196616 | tf_op jit(solution)/shard_map/ppermute | solution.py:24
  41.7 1.3 collective-permute-start.33
  46.5 1.5 multiply_convert_fusion.1
  48.0 6.2 %collective-permute-start.28 = (bf16[1,1,256,128]{3,2,1,0:T(8,128)(2,1)S(1)}, bf16[1,1,256,128]{3,2,1,0:T(8,128)(2,1)S(1)}, u32[]{:S(2)}, u32[]{:S(2)}) collective-permute-start(bf16[1,1,256,128]{3,2,1,0:T(8,128)(2,1)S(1)} %get-tuple-element.140), channel_id=1, source_target_pairs={{0,1},{1,2},{2,3},{3,4},{4,5},{5,6},{6,7},{8,9},{9,10},{10,11},{11... | collective-permute-start | bytes 196616 | tf_op jit(solution)/shard_map/ppermute | solution.py:24
  54.2 1.3 collective-permute-start.29
  58.1 3.0 fusion.7
  61.7 1.0 collective-permute-done.29
  69.0 103.8 %all-reduce.9.cloned.1.call-done = bf16[2,1152,128]{2,1,0:T(8,128)(2,1)} async-done(((bf16[2,1152,128]{2,1,0:T(8,128)(2,1)}), bf16[2,1152,128]{2,1,0:T(8,128)(2,1)}) %all-reduce.9.cloned.1.call-update) | async-done | bytes 589840 | tf_op jit(solution)/shard_map/psum | solution.py:101
  172.8 1.2 bitcast_subtract_fusion
  174.0 51.2 %conditional.2 = (f32[2,1152,128]{2,1,0:T(8,128)}, f32[1]{0:T(128)}) conditional(s32[]{:T(128)} %clamp.6, (f32[2,1152,128]{2,1,0:T(8,128)S(1)}, f32[1]{0:T(128)}) %tuple.56, (f32[2,1152,128]{2,1,0:T(8,128)S(1)}, f32[1]{0:T(128)}) %tuple.56, (f32[2,1152,128]{2,1,0:T(8,128)S(1)}, f32[1]{0:T(128)}) %tuple.56, ...), branch_computations={%region_1.2_spmd, %region_2.3_spmd, %region_3.4_spmd, %region_4.5_... | conditional | bytes 4718704 | solution.py:104
  174.0 5.7 %collective-permute-start.6 = (f32[2,1152,128]{2,1,0:T(8,128)S(1)}, f32[2,1152,128]{2,1,0:T(8,128)}, u32[]{:S(2)}, u32[]{:S(2)}) collective-permute-start(f32[2,1152,128]{2,1,0:T(8,128)S(1)} %get-tuple-element.54), channel_id=1, source_target_pairs={{0,64},{8,72},{16,80},{24,88},{32,96},{40,104},{48,112},{56,120},{... | collective-permute-start | bytes 3538952 | tf_op jit(solution)/shard_map/cond/branch_3_fun/ppermute | solution.py:14
  179.6 4.5 collective-permute-start.7
  184.1 41.1 %collective-permute-done.7 = f32[1]{0:T(128)} collective-permute-done((f32[1]{0:T(128)}, f32[1]{0:T(128)}, u32[]{:S(2)}, u32[]{:S(2)}) %collective-permute-start.7) | collective-permute-done | bytes 36 | tf_op jit(solution)/shard_map/cond/branch_3_fun/ppermute | solution.py:14
  225.9 1.4 divide_convert_fusion
  227.6 1.8 multiply_convert_fusion
  229.4 1.5 collective-permute-start.34
  230.9 1.3 collective-permute-start.35
  232.2 2.9 fusion.5
  235.2 3.6 collective-permute-done.35
  240.8 105.6 %all-reduce.11.cloned.1.call-done = bf16[2,1152,128]{2,1,0:T(8,128)(2,1)} async-done(((bf16[2,1152,128]{2,1,0:T(8,128)(2,1)}), bf16[2,1152,128]{2,1,0:T(8,128)(2,1)}) %all-reduce.11.cloned.1.call-update) | async-done | bytes 589840 | tf_op jit(solution)/shard_map/psum | solution.py:101
  346.3 1.6 multiply_subtract_fusion
  348.0 104.9 %conditional.3 = (f32[2,1152,128]{2,1,0:T(8,128)}, f32[1]{0:T(128)}) conditional(s32[]{:T(128)} %clamp.7, (f32[2,1152,128]{2,1,0:T(8,128)S(1)}, f32[1]{0:T(128)}) %tuple.57, (f32[2,1152,128]{2,1,0:T(8,128)S(1)}, f32[1]{0:T(128)}) %tuple.57, (f32[2,1152,128]{2,1,0:T(8,128)S(1)}, f32[1]{0:T(128)}) %tuple.57, ...), branch_computations={%region_8.9_spmd, %region_9.10_spmd, %region_10.11_spmd, %region_1... | conditional | bytes 4718704 | solution.py:104
  348.0 7.6 %collective-permute-start.20 = (f32[2,1152,128]{2,1,0:T(8,128)S(1)}, f32[2,1152,128]{2,1,0:T(8,128)}, u32[]{:S(2)}, u32[]{:S(2)}) collective-permute-start(f32[2,1152,128]{2,1,0:T(8,128)S(1)} %get-tuple-element.68), channel_id=1, source_target_pairs={{0,128},{8,136},{16,144},{24,152},{32,160},{40,168},{48,176},{56,1... | collective-permute-start | bytes 3538952 | tf_op jit(solution)/shard_map/cond/branch_4_fun/ppermute | solution.py:14
  355.7 96.4 %collective-permute-start.21 = (f32[1]{0:T(128)}, f32[1]{0:T(128)}, u32[]{:S(2)}, u32[]{:S(2)}) collective-permute-start(f32[1]{0:T(128)} %get-tuple-element.69), channel_id=1, source_target_pairs={{0,128},{8,136},{16,144},{24,152},{32,160},{40,168},{48,176},{56,1... | collective-permute-start | bytes 20 | tf_op jit(solution)/shard_map/cond/branch_4_fun/ppermute | solution.py:14
  453.6 2.4 multiply_bitcast_fusion
  (118 shorter events, 19.9 us)
Async XLA Ops:
  7.2 8.7 %copy-start.1 = (bf16[2,1,1,2,256,128]{5,4,3,2,1,0:T(8,128)(2,1)S(1)}, bf16[2,1,1,2,256,128]{5,4,3,2,1,0:T(8,128)(2,1)}, u32[]{:S(2)}) copy-start(bf16[2,1,1,2,256,128]{5,4,3,2,1,0:T(8,128)(2,1)} %param.17) | copy-start | bytes 786436
  7.2 24.1 %copy-start = (f32[1,2,1152,128]{3,2,1,0:T(8,128)S(1)}, f32[1,2,1152,128]{3,2,1,0:T(8,128)}, u32[]{:S(2)}) copy-start(f32[1,2,1152,128]{3,2,1,0:T(8,128)} %param.19) | copy-start | bytes 3538948
  7.2 165.6 %all-reduce.9.cloned.1.call-start = ((), (), s32[]{:S(2)}) async-start(), calls=%async_computation | async-start | bytes 1179648 | tf_op jit(solution)/shard_map/psum | solution.py:101
  9.0 24.0 %collective-permute-start.26 = (bf16[1,1,256,128]{3,2,1,0:T(8,128)(2,1)}, bf16[1,1,256,128]{3,2,1,0:T(8,128)(2,1)}, u32[]{:S(2)}, u32[]{:S(2)}) collective-permute-start(bf16[1,1,256,128]{3,2,1,0:T(8,128)(2,1)} %get-tuple-element.136), channel_id=1, source_target_pairs={{0,1},{1,2},{2,3},{3,4},{4,5},{5,6},{6,7},{8,9},{9,10},{10,11},{11... | collective-permute-start | bytes 196616 | tf_op jit(solution)/shard_map/ppermute | solution.py:24
  14.6 19.8 %collective-permute-start.27 = (bf16[1,1,256,128]{3,2,1,0:T(8,128)(2,1)}, bf16[1,1,256,128]{3,2,1,0:T(8,128)(2,1)}, u32[]{:S(2)}, u32[]{:S(2)}) collective-permute-start(bf16[1,1,256,128]{3,2,1,0:T(8,128)(2,1)} %get-tuple-element.137), channel_id=1, source_target_pairs={{1,0},{2,1},{3,2},{4,3},{5,4},{6,5},{7,6},{9,8},{10,9},{11,10},{12... | collective-permute-start | bytes 196616 | tf_op jit(solution)/shard_map/ppermute | solution.py:25
  16.6 25.1 %collective-permute-start.24 = (bf16[1,1,256,128]{3,2,1,0:T(8,128)(2,1)}, bf16[1,1,256,128]{3,2,1,0:T(8,128)(2,1)S(1)}, u32[]{:S(2)}, u32[]{:S(2)}) collective-permute-start(bf16[1,1,256,128]{3,2,1,0:T(8,128)(2,1)} %get-tuple-element.144), channel_id=1, source_target_pairs={{0,1},{1,2},{2,3},{3,4},{4,5},{5,6},{6,7},{8,9},{9,10},{10,11},{11... | collective-permute-start | bytes 196616 | tf_op jit(solution)/shard_map/ppermute | solution.py:24
  22.7 20.3 %collective-permute-start.25 = (bf16[1,1,256,128]{3,2,1,0:T(8,128)(2,1)}, bf16[1,1,256,128]{3,2,1,0:T(8,128)(2,1)}, u32[]{:S(2)}, u32[]{:S(2)}) collective-permute-start(bf16[1,1,256,128]{3,2,1,0:T(8,128)(2,1)} %get-tuple-element.145), channel_id=1, source_target_pairs={{1,0},{2,1},{3,2},{4,3},{5,4},{6,5},{7,6},{9,8},{10,9},{11,10},{12... | collective-permute-start | bytes 196616 | tf_op jit(solution)/shard_map/ppermute | solution.py:25
  24.6 29.6 %collective-permute-start.30 = (bf16[1,1,256,128]{3,2,1,0:T(8,128)(2,1)}, bf16[1,1,256,128]{3,2,1,0:T(8,128)(2,1)S(1)}, u32[]{:S(2)}, u32[]{:S(2)}) collective-permute-start(bf16[1,1,256,128]{3,2,1,0:T(8,128)(2,1)} %get-tuple-element.148), channel_id=1, source_target_pairs={{0,1},{1,2},{2,3},{3,4},{4,5},{5,6},{6,7},{8,9},{9,10},{10,11},{11... | collective-permute-start | bytes 196616 | tf_op jit(solution)/shard_map/ppermute | solution.py:24
  33.0 22.5 %collective-permute-start.31 = (bf16[1,1,256,128]{3,2,1,0:T(8,128)(2,1)}, bf16[1,1,256,128]{3,2,1,0:T(8,128)(2,1)S(1)}, u32[]{:S(2)}, u32[]{:S(2)}) collective-permute-start(bf16[1,1,256,128]{3,2,1,0:T(8,128)(2,1)} %get-tuple-element.149), channel_id=1, source_target_pairs={{1,0},{2,1},{3,2},{4,3},{5,4},{6,5},{7,6},{9,8},{10,9},{11,10},{12... | collective-permute-start | bytes 196616 | tf_op jit(solution)/shard_map/ppermute | solution.py:25
  34.4 7.3 %copy-start.2 = (bf16[1,1,256,128]{3,2,1,0:T(8,128)(2,1)S(1)}, bf16[1,1,256,128]{3,2,1,0:T(8,128)(2,1)}, u32[]{:S(2)}) copy-start(bf16[1,1,256,128]{3,2,1,0:T(8,128)(2,1)} %get-tuple-element.129) | copy-start | bytes 196612
  34.4 21.4 %collective-permute-start.32 = (bf16[1,1,256,128]{3,2,1,0:T(8,128)(2,1)}, bf16[1,1,256,128]{3,2,1,0:T(8,128)(2,1)S(1)}, u32[]{:S(2)}, u32[]{:S(2)}) collective-permute-start(bf16[1,1,256,128]{3,2,1,0:T(8,128)(2,1)} %get-tuple-element.128), channel_id=1, source_target_pairs={{0,1},{1,2},{2,3},{3,4},{4,5},{5,6},{6,7},{8,9},{9,10},{10,11},{11... | collective-permute-start | bytes 196616 | tf_op jit(solution)/shard_map/ppermute | solution.py:24
  41.7 14.1 %collective-permute-start.33 = (bf16[1,1,256,128]{3,2,1,0:T(8,128)(2,1)S(1)}, bf16[1,1,256,128]{3,2,1,0:T(8,128)(2,1)S(1)}, u32[]{:S(2)}, u32[]{:S(2)}) collective-permute-start(bf16[1,1,256,128]{3,2,1,0:T(8,128)(2,1)S(1)} %copy-done.2), channel_id=1, source_target_pairs={{1,0},{2,1},{3,2},{4,3},{5,4},{6,5},{7,6},{9,8},{10,9},{11,10},{12... | collective-permute-start | bytes 196616 | tf_op jit(solution)/shard_map/ppermute | solution.py:25
  46.5 1.5 copy-start.3
  46.5 1.5 copy-start.4
  48.0 13.7 %collective-permute-start.28 = (bf16[1,1,256,128]{3,2,1,0:T(8,128)(2,1)S(1)}, bf16[1,1,256,128]{3,2,1,0:T(8,128)(2,1)S(1)}, u32[]{:S(2)}, u32[]{:S(2)}) collective-permute-start(bf16[1,1,256,128]{3,2,1,0:T(8,128)(2,1)S(1)} %get-tuple-element.140), channel_id=1, source_target_pairs={{0,1},{1,2},{2,3},{3,4},{4,5},{5,6},{6,7},{8,9},{9,10},{10,11},{11... | collective-permute-start | bytes 196616 | tf_op jit(solution)/shard_map/ppermute | solution.py:24
  54.2 8.6 %collective-permute-start.29 = (bf16[1,1,256,128]{3,2,1,0:T(8,128)(2,1)S(1)}, bf16[1,1,256,128]{3,2,1,0:T(8,128)(2,1)S(1)}, u32[]{:S(2)}, u32[]{:S(2)}) collective-permute-start(bf16[1,1,256,128]{3,2,1,0:T(8,128)(2,1)S(1)} %get-tuple-element.141), channel_id=1, source_target_pairs={{1,0},{2,1},{3,2},{4,3},{5,4},{6,5},{7,6},{9,8},{10,9},{11,10},{12... | collective-permute-start | bytes 196616 | tf_op jit(solution)/shard_map/ppermute | solution.py:25
  57.0 1.1 copy-start.5
  64.8 281.5 %all-reduce.11.cloned.1.call-start = ((), (), s32[]{:S(2)}) async-start(), calls=%async_computation.1 | async-start | bytes 1179648 | tf_op jit(solution)/shard_map/psum | solution.py:101
  174.0 51.2 %collective-permute-start.6 = (f32[2,1152,128]{2,1,0:T(8,128)S(1)}, f32[2,1152,128]{2,1,0:T(8,128)}, u32[]{:S(2)}, u32[]{:S(2)}) collective-permute-start(f32[2,1152,128]{2,1,0:T(8,128)S(1)} %get-tuple-element.54), channel_id=1, source_target_pairs={{0,64},{8,72},{16,80},{24,88},{32,96},{40,104},{48,112},{56,120},{... | collective-permute-start | bytes 3538952 | tf_op jit(solution)/shard_map/cond/branch_3_fun/ppermute | solution.py:14
  179.6 45.5 %collective-permute-start.7 = (f32[1]{0:T(128)}, f32[1]{0:T(128)}, u32[]{:S(2)}, u32[]{:S(2)}) collective-permute-start(f32[1]{0:T(128)} %get-tuple-element.55), channel_id=1, source_target_pairs={{0,64},{8,72},{16,80},{24,88},{32,96},{40,104},{48,112},{56,120},{... | collective-permute-start | bytes 20 | tf_op jit(solution)/shard_map/cond/branch_3_fun/ppermute | solution.py:14
  229.4 5.8 %collective-permute-start.34 = (bf16[1,1,256,128]{3,2,1,0:T(8,128)(2,1)S(1)}, bf16[1,1,256,128]{3,2,1,0:T(8,128)(2,1)S(1)}, u32[]{:S(2)}, u32[]{:S(2)}) collective-permute-start(bf16[1,1,256,128]{3,2,1,0:T(8,128)(2,1)S(1)} %get-tuple-element.132), channel_id=1, source_target_pairs={{0,1},{1,2},{2,3},{3,4},{4,5},{5,6},{6,7},{8,9},{9,10},{10,11},{11... | collective-permute-start | bytes 196616 | tf_op jit(solution)/shard_map/ppermute | solution.py:24
  230.9 7.8 %collective-permute-start.35 = (bf16[1,1,256,128]{3,2,1,0:T(8,128)(2,1)S(1)}, bf16[1,1,256,128]{3,2,1,0:T(8,128)(2,1)S(1)}, u32[]{:S(2)}, u32[]{:S(2)}) collective-permute-start(bf16[1,1,256,128]{3,2,1,0:T(8,128)(2,1)S(1)} %get-tuple-element.133), channel_id=1, source_target_pairs={{1,0},{2,1},{3,2},{4,3},{5,4},{6,5},{7,6},{9,8},{10,9},{11,10},{12... | collective-permute-start | bytes 196616 | tf_op jit(solution)/shard_map/ppermute | solution.py:25
  348.0 104.9 %collective-permute-start.20 = (f32[2,1152,128]{2,1,0:T(8,128)S(1)}, f32[2,1152,128]{2,1,0:T(8,128)}, u32[]{:S(2)}, u32[]{:S(2)}) collective-permute-start(f32[2,1152,128]{2,1,0:T(8,128)S(1)} %get-tuple-element.68), channel_id=1, source_target_pairs={{0,128},{8,136},{16,144},{24,152},{32,160},{40,168},{48,176},{56,1... | collective-permute-start | bytes 3538952 | tf_op jit(solution)/shard_map/cond/branch_4_fun/ppermute | solution.py:14
  355.7 97.2 %collective-permute-start.21 = (f32[1]{0:T(128)}, f32[1]{0:T(128)}, u32[]{:S(2)}, u32[]{:S(2)}) collective-permute-start(f32[1]{0:T(128)} %get-tuple-element.69), channel_id=1, source_target_pairs={{0,128},{8,136},{16,144},{24,152},{32,160},{40,168},{48,176},{56,1... | collective-permute-start | bytes 20 | tf_op jit(solution)/shard_map/cond/branch_4_fun/ppermute | solution.py:14
Sparse Core Ops, SparseCore 0:
  64.9 107.7 all-reduce.8
  240.9 105.4 all-reduce.10
where the time goes:
time: 465 us; the launch traced here: 464 us
  waiting for transfers between devices  256 us (55%)
  starting transfers between devices  153 us (33%)
  between operations  18.6 us (4%)
  local copies, waits for them, and re-layouts  13.1 us (3%)
  other arithmetic  12.6 us (3%)
  matrix products  10.2 us (2%)
    psum x2, waiting for transfers between devices, shards(): lax.psum(local_grads.astype(jnp.bfloat16), 'tile').astype(jnp.float32)  209 us
    ppermute x4, starting transfers between devices, passed_along(): lax.ppermute(shard, axis, [(i, (i + by) % devices) for i in range(devices)])  114 us
    ppermute x4, waiting for transfers between devices, passed_along(): lax.ppermute(shard, axis, [(i, (i + by) % devices) for i in range(devices)])  41.9 us
    ppermute x6, starting transfers between devices, with_halo(): before = lax.ppermute(last, axis, up)  31.5 us
  transfers between devices with their start and end apart: 18, of which 6 were waited for; matrix products, arithmetic and copies ran while one was open for 5% of the time, Pallas kernels for 0%

commit v1 on v0

v1 whole, which is shorter than its diff:
```python
from functools import partial
import math

import jax
import jax.numpy as jnp
from jax import lax
from jax.sharding import PartitionSpec as P

learn_rate = 0.03


def passed_along(shard, axis, by):
    devices = lax.axis_size(axis)
    return lax.ppermute(shard, axis, [(i, (i + by) % devices) for i in range(devices)])


def pushed(payload, level):
    levels = lax.axis_size("rep").bit_length() - 1
    branches = [partial(passed_along, axis="rep", by=1 << bit_num) for bit_num in range(levels)]
    return lax.switch(level, branches, payload)


def pad_columns(field_in):
    return jnp.pad(field_in, ((0, 0), (0, 0), (1, 1), (0, 0)))


def patches(padded):
    out_rows = padded.shape[1] - 2
    out_cols = padded.shape[2] - 2
    pieces = [
        padded[:, row_off : row_off + out_rows, col_off : col_off + out_cols, :]
        for row_off in range(3)
        for col_off in range(3)
    ]
    return jnp.concatenate(pieces, axis=-1).reshape(-1, 9 * padded.shape[3])


def flipped(kernel):
    channels = kernel.shape[1]
    return (
        kernel.reshape(3, 3, channels, channels)[::-1, ::-1]
        .transpose(0, 1, 3, 2)
        .reshape(9 * channels, channels)
    )


def contract_rows(left_mat, right_mat):
    return lax.dot_general(
        left_mat, right_mat, (((0,), (0,)), ((), ())), preferred_element_type=jnp.float32
    )


def halo_rows(images, out_grads):
    tiles = lax.axis_size("tile")
    own_rows = images.shape[3]
    for_below = jnp.concatenate([images[:, 0], out_grads[:, 0, :, own_rows - 1 :]], axis=2)
    for_above = jnp.concatenate([images[:, 0], out_grads[:, 0, :, :1]], axis=2)
    down = [(i, i + 1) for i in range(tiles - 1)]
    up = [(i + 1, i) for i in range(tiles - 1)]
    return lax.ppermute(for_below, "tile", down), lax.ppermute(for_above, "tile", up)


def local_grads(x_ext, g_ext, weights, first, last):
    batch_size, ext_rows, columns, channels = x_ext.shape
    own_rows = ext_rows - 4
    norm_scale = 1.0 / math.sqrt(9 * channels)
    input_patches = patches(pad_columns(x_ext))
    pre_ext = norm_scale * jnp.dot(input_patches, weights[0], preferred_element_type=jnp.float32)
    pre_ext = pre_ext.reshape(batch_size, own_rows + 2, columns, channels)
    row_ids = lax.broadcasted_iota(jnp.int32, (1, own_rows + 2, 1, 1), 1)
    outside = ((row_ids == 0) & first) | ((row_ids == own_rows + 1) & last)
    hidden_ext = jnp.where(outside, 0.0, jax.nn.silu(pre_ext)).astype(jnp.bfloat16)
    pre_act = pre_ext[:, 1 : own_rows + 1].reshape(-1, channels)
    own_input_patches = input_patches.reshape(batch_size, own_rows + 2, columns, -1)[
        :, 1 : own_rows + 1
    ].reshape(-1, 9 * channels)
    hidden_patches = patches(pad_columns(hidden_ext))
    grad_patches = patches(pad_columns(g_ext))
    grad_hidden = norm_scale * jnp.dot(
        grad_patches, flipped(weights[1]), preferred_element_type=jnp.float32
    )
    sigmoid_val = jax.nn.sigmoid(pre_act)
    grad_pre = (grad_hidden * sigmoid_val * (1.0 + pre_act * (1.0 - sigmoid_val))).astype(
        jnp.bfloat16
    )
    grad_own = g_ext[:, 1 : own_rows + 1].reshape(-1, channels)
    first_grad = norm_scale * contract_rows(own_input_patches, grad_pre)
    second = norm_scale * contract_rows(hidden_patches, grad_own)
    return jnp.stack([first_grad, second])


def scattered_sum(grads, tiles):
    chunks = grads.astype(jnp.bfloat16).reshape(tiles, -1, grads.shape[-1])
    got = lax.all_to_all(chunks, "tile", 0, 0, tiled=True)
    return got.astype(jnp.float32).sum(0)


def gathered(chunk, tiles):
    spread = jnp.broadcast_to(chunk[None], (tiles,) + chunk.shape)
    return lax.all_to_all(spread, "tile", 0, 0, tiled=True)


def with_weight(chunk, weight):
    return jnp.concatenate([chunk, jnp.broadcast_to(weight, (1, chunk.shape[-1]))], axis=0)


def shards(images, out_grads, numerators, push_weight, step_index):
    levels = lax.axis_size("rep").bit_length() - 1
    tiles = lax.axis_size("tile")
    tile = lax.axis_index("tile")
    first, last = tile == 0, tile == tiles - 1
    kernel_shape = numerators.shape[1:]
    channels = kernel_shape[-1]
    full_state = numerators[0]
    state_rows = full_state.size // (tiles * channels)
    sum_state = full_state.reshape(tiles, state_rows, channels)[tile]
    weight = push_weight[0]
    above, below = halo_rows(images, out_grads)
    own_rows = images.shape[3]
    got = pushed(with_weight(sum_state, weight), step_index[0] % levels)
    for step_num in range(images.shape[0]):
        peer_level = (step_index[0] + step_num) % levels
        if step_num == 0:
            weights = (full_state / weight).astype(jnp.bfloat16)
        else:
            weights = gathered((sum_state / weight).astype(jnp.bfloat16), tiles).reshape(
                kernel_shape
            )
            got = pushed(with_weight(sum_state, weight), peer_level)
        x_ext = jnp.concatenate(
            [above[step_num][:, :own_rows], images[step_num, 0], below[step_num][:, :own_rows]],
            axis=1,
        )
        g_ext = jnp.concatenate(
            [above[step_num][:, own_rows:], out_grads[step_num, 0], below[step_num][:, own_rows:]],
            axis=1,
        )
        grads_chunk = scattered_sum(local_grads(x_ext, g_ext, weights, first, last), tiles)
        peer_grads = pushed(grads_chunk, peer_level)
        own_part = sum_state - learn_rate * grads_chunk
        peer_part = got[:state_rows] - learn_rate * peer_grads
        sum_state = 0.5 * (own_part + peer_part)
        weight = 0.5 * (weight + got[state_rows, 0])
    new_state = gathered(sum_state, tiles).reshape(kernel_shape)
    return (new_state[None], jnp.reshape(weight, (1,)))


def solution(mesh):
    in_specs = (
        P(None, "rep", None, "tile", None, None),
        P(None, "rep", None, "tile", None, None),
        P("rep", None, None, None),
        P("rep"),
        P(),
    )
    out_specs = (P("rep", None, None, None), P("rep"))
    return jax.shard_map(shards, mesh=mesh, in_specs=in_specs, out_specs=out_specs, check_vma=False)
```

time: 465 us -> 171 us (0.37)
  the two profiles are of different devices: /device:TPU:96 before, /device:TPU:32 now
where the time goes in v1:
time: 171 us; the launch traced here: 170 us
  waiting for transfers between devices  64.7 us (38%)
  starting transfers between devices  57.2 us (33%)
  local copies, waits for them, and re-layouts  23.1 us (14%)
  other arithmetic  10.7 us (6%)
  matrix products  9.12 us (5%)
  between operations  4.97 us (3%)
    ppermute x4, waiting for transfers between devices, passed_along(): lax.ppermute(shard, axis, [(i, (i + by) % devices) for i in range(devices)])  32.8 us
    ppermute x4, starting transfers between devices, passed_along(): lax.ppermute(shard, axis, [(i, (i + by) % devices) for i in range(devices)])  31.1 us
    all_to_all x2, waiting for transfers between devices, gathered(): return lax.all_to_all(spread, 'tile', 0, 0, tiled=True)  21.4 us
    all_to_all x2, starting transfers between devices, scattered_sum(): got = lax.all_to_all(chunks, 'tile', 0, 0, tiled=True)  10.8 us
    all_to_all x2, waiting for transfers between devices, scattered_sum(): got = lax.all_to_all(chunks, 'tile', 0, 0, tiled=True)  10.5 us
    unnamed x73, local copies, waits for them, and re-layouts  9.57 us
    dot_general x4, matrix products, contract_rows(): lax.dot_general(left_mat, right_mat, (((0,), (0,)), ((), ())), preferred_...  7.55 us
    all_to_all x2, starting transfers between devices, gathered(): return lax.all_to_all(spread, 'tile', 0, 0, tiled=True)  7.15 us
  transfers between devices with their start and end apart: 10, of which 8 were waited for; matrix products, arithmetic and copies ran while one was open for 9% of the time, Pallas kernels for 0%

profile of v1, /device:TPU:32, one launch (start us, length us, event | category | flops | bytes accessed | tf_op | source)
XLA Modules:
  0.0 170.0 jit_solution(1175194113306961317)
XLA Ops:
  0.7 1.1 slice_bitcast_fusion.9
  1.8 1.9 %pad_maximum_fusion.3 = (bf16[2,1,3,256,128]{4,3,2,1,0:T(8,128)(2,1)}, bf16[2,1,3,256,128]{4,3,2,1,0:T(8,128)(2,1)}) fusion(bf16[2,1,2,256,128]{4,3,2,1,0:T(8,128)(2,1)} %bitcast.148, bf16[2,1,1,256,128]{4,3,2,1,0:T(8,128)(2,1)S(1)} %get-tuple-element.110, bf16[2,1,1,256,128]{4,3,2,1,0:T(8,128)(2,1)S(1)} %get-tuple-element.111), kind=kLoop, calls=%fused_computation.33 | loop fusion | flops 393216 | bytes 1310720 | tf_op jit(solution)/shard_map/concatenate | solution.py:56
  3.7 1.4 collective-permute-start.25
  5.1 6.8 %collective-permute-start.24 = (bf16[2,1,3,256,128]{4,3,2,1,0:T(8,128)(2,1)}, bf16[2,1,3,256,128]{4,3,2,1,0:T(8,128)(2,1)}, u32[]{:S(2)}, u32[]{:S(2)}) collective-permute-start(bf16[2,1,3,256,128]{4,3,2,1,0:T(8,128)(2,1)} %get-tuple-element.108), channel_id=1, source_target_pairs={{0,1},{1,2},{2,3},{3,4},{4,5},{5,6},{6,7},{8,9},{9,10},{10,11},{11... | collective-permute-start | bytes 1179656 | tf_op jit(solution)/shard_map/ppermute | solution.py:60
  14.2 28.4 %conditional.4 = (f32[289,128]{1,0:T(8,128)}) conditional(s32[]{:T(128)} %clamp.8, (f32[288,128]{1,0:T(8,128)S(1)}, f32[]{:T(128)}) %tuple.81, (f32[288,128]{1,0:T(8,128)S(1)}, f32[]{:T(128)}) %tuple.81, (f32[288,128]{1,0:T(8,128)S(1)}, f32[]{:T(128)}) %tuple.81, (f32[288,128]{1,0:T(8,128)S(1)}, f32[]{:T(128)}) %tuple.81, ...), branch_computations={%region_1.2_spmd, %region_2.3_spmd, %region_3.4_spmd, %region_4.5_... | conditional | bytes 887348 | solution.py:20
  14.9 14.8 %collective-permute-start.5 = (f32[289,128]{1,0:T(8,128)S(1)}, f32[289,128]{1,0:T(8,128)}, u32[]{:S(2)}, u32[]{:S(2)}) collective-permute-start(f32[289,128]{1,0:T(8,128)S(1)} %concatenate.185), channel_id=1, source_target_pairs={{0,256},{8,264},{16,272},{24,280},{32,288},{40,296},{48,304},{56,3... | collective-permute-start | bytes 443912 | tf_op jit(solution)/shard_map/cond/branch_5_fun/ppermute | solution.py:14
  29.7 12.9 %collective-permute-done.5 = f32[289,128]{1,0:T(8,128)} collective-permute-done((f32[289,128]{1,0:T(8,128)S(1)}, f32[289,128]{1,0:T(8,128)}, u32[]{:S(2)}, u32[]{:S(2)}) %collective-permute-start.5) | collective-permute-done | bytes 148000 | tf_op jit(solution)/shard_map/cond/branch_5_fun/ppermute | solution.py:14
  42.6 1.2 slice.387
  52.0 1.3 fusion.6
  53.6 3.2 %fusion.7 = bf16[1,1152,128]{2,1,0:T(8,128)(2,1)} fusion(bf16[512,1152]{1,0:T(8,128)(2,1)S(1)} %bitcast.132, f32[512,128]{1,0:T(8,128)} %get-tuple-element.107, f32[512,128]{1,0:T(8,128)} %get-tuple-element.106, bf16[512,1152]{1,0:T(8,128)(2,1)S(1)} %constant_dynamic-update-slice_fusion, bf16[1152,128]{1,0:T(8,128)(2,1)} %bitcast.144), kind=kOutput, calls=%fused_computation.11 | convolution fusion | flops 302546944 | bytes 3473408 | tf_op jit(solution)/shard_map/dot_general | solution.py:48
  56.8 1.9 %pad_maximum_fusion = bf16[2,1152,128]{2,1,0:T(8,128)(2,1)} fusion(bf16[1,1152,128]{2,1,0:T(8,128)(2,1)} %fusion.6, bf16[1,1152,128]{2,1,0:T(8,128)(2,1)} %fusion.7), kind=kLoop, calls=%fused_computation.27 | loop fusion | flops 294912 | bytes 1179648 | tf_op jit(solution)/shard_map/stack | solution.py:89
  58.7 7.2 %all-to-all-start = ((bf16[8,288,128]{2,1,0:T(8,128)(2,1)}), bf16[8,288,128]{2,1,0:T(8,128)(2,1)}, u32[]{:S(2)}, u32[]{:S(2)}) async-start(bf16[8,288,128]{2,1,0:T(8,128)(2,1)} %bitcast.32), calls=%async_computation | async-start | bytes 1179648 | tf_op jit(solution)/shard_map/all_to_all | solution.py:94
  70.4 6.9 %all-to-all-done = bf16[8,288,128]{2,1,0:T(8,128)(2,1)} async-done(((bf16[8,288,128]{2,1,0:T(8,128)(2,1)}), bf16[8,288,128]{2,1,0:T(8,128)(2,1)}, u32[]{:S(2)}, u32[]{:S(2)}) %all-to-all-start) | async-done | bytes 589856 | tf_op jit(solution)/shard_map/all_to_all | solution.py:94
  77.3 1.2 convert_reduce_fusion.1
  78.4 21.3 %conditional.5 = (f32[288,128]{1,0:T(8,128)}) conditional(s32[]{:T(128)} %clamp.8, f32[288,128]{1,0:T(8,128)S(1)} %convert_reduce_fusion.1, f32[288,128]{1,0:T(8,128)S(1)} %convert_reduce_fusion.1, f32[288,128]{1,0:T(8,128)S(1)} %convert_reduce_fusion.1, f32[288,128]{1,0:T(8,128)S(1)} %convert_reduce_fusion.1, ...), branch_computations={%region_7.8_spmd, %region_8.9_spmd, %region_9.10_spmd, %region_10.... | conditional | bytes 589872 | solution.py:20
  78.5 12.4 %collective-permute-start.11 = (f32[288,128]{1,0:T(8,128)S(1)}, f32[288,128]{1,0:T(8,128)}, u32[]{:S(2)}, u32[]{:S(2)}) collective-permute-start(f32[288,128]{1,0:T(8,128)S(1)} %param.11), channel_id=1, source_target_pairs={{0,256},{8,264},{16,272},{24,280},{32,288},{40,296},{48,304},{56,3... | collective-permute-start | bytes 442376 | tf_op jit(solution)/shard_map/cond/branch_5_fun/ppermute | solution.py:14
  90.9 8.8 %collective-permute-done.11 = f32[288,128]{1,0:T(8,128)} collective-permute-done((f32[288,128]{1,0:T(8,128)S(1)}, f32[288,128]{1,0:T(8,128)}, u32[]{:S(2)}, u32[]{:S(2)}) %collective-permute-start.11) | collective-permute-done | bytes 147488 | tf_op jit(solution)/shard_map/cond/branch_5_fun/ppermute | solution.py:14
  101.7 3.5 %all-to-all-start.1 = ((bf16[8,288,128]{2,1,0:T(8,128)(2,1)}), bf16[8,288,128]{2,1,0:T(8,128)(2,1)S(1)}, u32[]{:S(2)}, u32[]{:S(2)}) async-start(bf16[8,288,128]{2,1,0:T(8,128)(2,1)} %broadcast_in_dim.32), calls=%async_computation.1 | async-start | bytes 1179648 | tf_op jit(solution)/shard_map/all_to_all | solution.py:100
  105.9 1.1 slice.378
  109.8 6.0 %all-to-all-done.1 = bf16[8,288,128]{2,1,0:T(8,128)(2,1)S(1)} async-done(((bf16[8,288,128]{2,1,0:T(8,128)(2,1)}), bf16[8,288,128]{2,1,0:T(8,128)(2,1)S(1)}, u32[]{:S(2)}, u32[]{:S(2)}) %all-to-all-start.1) | async-done | bytes 589856 | tf_op jit(solution)/shard_map/all_to_all | solution.py:100
  119.1 2.6 %fusion.5 = bf16[1,1152,128]{2,1,0:T(8,128)(2,1)S(1)} fusion(bf16[512,1152]{1,0:T(8,128)(2,1)S(1)} %bitcast.133, f32[512,128]{1,0:T(8,128)S(1)} %get-tuple-element.103, f32[512,128]{1,0:T(8,128)S(1)} %get-tuple-element.102, bf16[512,1152]{1,0:T(8,128)(2,1)} %constant_dynamic-update-slice_fusion.9, bf16[1152,128]{1,0:T(8,128)(2,1)S(1)} %bitcast.146), kind=kOutput, calls=%fused_computation.9 | convolution fusion | flops 302546944 | bytes 3473408 | tf_op jit(solution)/shard_map/dot_general | solution.py:48
  122.6 3.5 %all-to-all-start.2 = ((bf16[8,288,128]{2,1,0:T(8,128)(2,1)}), bf16[8,288,128]{2,1,0:T(8,128)(2,1)S(1)}, u32[]{:S(2)}, u32[]{:S(2)}) async-start(bf16[8,288,128]{2,1,0:T(8,128)(2,1)} %bitcast.59), calls=%async_computation.2 | async-start | bytes 1179648 | tf_op jit(solution)/shard_map/all_to_all | solution.py:94
  126.2 7.5 %conditional.6 = (f32[289,128]{1,0:T(8,128)}) conditional(s32[]{:T(128)} %clamp.9, (f32[288,128]{1,0:T(8,128)S(1)}, f32[]{:T(128)}) %tuple.82, (f32[288,128]{1,0:T(8,128)S(1)}, f32[]{:T(128)}) %tuple.82, (f32[288,128]{1,0:T(8,128)S(1)}, f32[]{:T(128)}) %tuple.82, (f32[288,128]{1,0:T(8,128)S(1)}, f32[]{:T(128)}) %tuple.82, ...), branch_computations={%region_14.15_spmd, %region_15.16_spmd, %region_16.17_spmd, %regio... | conditional | bytes 887348 | solution.py:20
  126.2 1.9 %collective-permute-start.12 = (f32[289,128]{1,0:T(8,128)S(1)}, f32[289,128]{1,0:T(8,128)}, u32[]{:S(2)}, u32[]{:S(2)}) collective-permute-start(f32[289,128]{1,0:T(8,128)S(1)} %concatenate.186), channel_id=1, source_target_pairs={{0,8},{8,16},{16,24},{24,32},{32,40},{40,48},{48,56},{56,64},{64,7... | collective-permute-start | bytes 443912 | tf_op jit(solution)/shard_map/cond/branch_0_fun/ppermute | solution.py:14
  128.1 5.6 %collective-permute-done.12 = f32[289,128]{1,0:T(8,128)} collective-permute-done((f32[289,128]{1,0:T(8,128)S(1)}, f32[289,128]{1,0:T(8,128)}, u32[]{:S(2)}, u32[]{:S(2)}) %collective-permute-start.12) | collective-permute-done | bytes 148000 | tf_op jit(solution)/shard_map/cond/branch_0_fun/ppermute | solution.py:14
  133.7 3.6 %all-to-all-done.2 = bf16[8,288,128]{2,1,0:T(8,128)(2,1)S(1)} async-done(((bf16[8,288,128]{2,1,0:T(8,128)(2,1)}), bf16[8,288,128]{2,1,0:T(8,128)(2,1)S(1)}, u32[]{:S(2)}, u32[]{:S(2)}) %all-to-all-start.2) | async-done | bytes 589856 | tf_op jit(solution)/shard_map/all_to_all | solution.py:94
  137.4 7.5 %conditional.7 = (f32[288,128]{1,0:T(8,128)}) conditional(s32[]{:T(128)} %clamp.9, f32[288,128]{1,0:T(8,128)S(1)} %convert_reduce_fusion, f32[288,128]{1,0:T(8,128)S(1)} %convert_reduce_fusion, f32[288,128]{1,0:T(8,128)S(1)} %convert_reduce_fusion, f32[288,128]{1,0:T(8,128)S(1)} %convert_reduce_fusion, ...), branch_computations={%region_20.21_spmd, %region_21.22_spmd, %region_22.23_spmd, %regio... | conditional | bytes 589872 | solution.py:20
  137.4 1.9 %collective-permute-start.18 = (f32[288,128]{1,0:T(8,128)S(1)}, f32[288,128]{1,0:T(8,128)}, u32[]{:S(2)}, u32[]{:S(2)}) collective-permute-start(f32[288,128]{1,0:T(8,128)S(1)} %param.18), channel_id=1, source_target_pairs={{0,8},{8,16},{16,24},{24,32},{32,40},{40,48},{48,56},{56,64},{64,7... | collective-permute-start | bytes 442376 | tf_op jit(solution)/shard_map/cond/branch_0_fun/ppermute | solution.py:14
  139.3 5.5 %collective-permute-done.18 = f32[288,128]{1,0:T(8,128)} collective-permute-done((f32[288,128]{1,0:T(8,128)S(1)}, f32[288,128]{1,0:T(8,128)}, u32[]{:S(2)}, u32[]{:S(2)}) %collective-permute-start.18) | collective-permute-done | bytes 147488 | tf_op jit(solution)/shard_map/cond/branch_0_fun/ppermute | solution.py:14
  147.0 3.6 %all-to-all-start.3 = ((f32[8,288,128]{2,1,0:T(8,128)}), f32[8,288,128]{2,1,0:T(8,128)S(1)}, u32[]{:S(2)}, u32[]{:S(2)}) async-start(f32[8,288,128]{2,1,0:T(8,128)} %broadcast_in_dim.33), calls=%async_computation.3 | async-start | bytes 2359296 | tf_op jit(solution)/shard_map/all_to_all | solution.py:100
  150.6 1.2 slice.395
  152.4 15.4 %all-to-all-done.3 = f32[8,288,128]{2,1,0:T(8,128)S(1)} async-done(((f32[8,288,128]{2,1,0:T(8,128)}), f32[8,288,128]{2,1,0:T(8,128)S(1)}, u32[]{:S(2)}, u32[]{:S(2)}) %all-to-all-start.3) | async-done | bytes 1179680 | tf_op jit(solution)/shard_map/all_to_all | solution.py:100
  (129 shorter events, 26.3 us)
Async XLA Ops:
  0.6 11.3 %copy-start.7 = (bf16[2,1,1,2,256,128]{5,4,3,2,1,0:T(8,128)(2,1)S(1)}, bf16[2,1,1,2,256,128]{5,4,3,2,1,0:T(8,128)(2,1)}, u32[]{:S(2)}) copy-start(bf16[2,1,1,2,256,128]{5,4,3,2,1,0:T(8,128)(2,1)} %param.29) | copy-start | bytes 786436
  0.6 11.9 %copy-start.1 = (f32[1,2,1152,128]{3,2,1,0:T(8,128)S(1)}, f32[1,2,1152,128]{3,2,1,0:T(8,128)}, u32[]{:S(2)}) copy-start(f32[1,2,1152,128]{3,2,1,0:T(8,128)} %param.31) | copy-start | bytes 3538948
  3.7 9.0 %copy-start.8 = (bf16[2,1,1,2,256,128]{5,4,3,2,1,0:T(8,128)(2,1)S(1)}, bf16[2,1,1,2,256,128]{5,4,3,2,1,0:T(8,128)(2,1)}, u32[]{:S(2)}) copy-start(bf16[2,1,1,2,256,128]{5,4,3,2,1,0:T(8,128)(2,1)} %param.30) | copy-start | bytes 786436
  3.7 41.6 %collective-permute-start.25 = (bf16[2,1,3,256,128]{4,3,2,1,0:T(8,128)(2,1)}, bf16[2,1,3,256,128]{4,3,2,1,0:T(8,128)(2,1)}, u32[]{:S(2)}, u32[]{:S(2)}) collective-permute-start(bf16[2,1,3,256,128]{4,3,2,1,0:T(8,128)(2,1)} %get-tuple-element.109), channel_id=1, source_target_pairs={{1,0},{2,1},{3,2},{4,3},{5,4},{6,5},{7,6},{9,8},{10,9},{11,10},{12... | collective-permute-start | bytes 1179656 | tf_op jit(solution)/shard_map/ppermute | solution.py:60
  5.1 41.3 %collective-permute-start.24 = (bf16[2,1,3,256,128]{4,3,2,1,0:T(8,128)(2,1)}, bf16[2,1,3,256,128]{4,3,2,1,0:T(8,128)(2,1)}, u32[]{:S(2)}, u32[]{:S(2)}) collective-permute-start(bf16[2,1,3,256,128]{4,3,2,1,0:T(8,128)(2,1)} %get-tuple-element.108), channel_id=1, source_target_pairs={{0,1},{1,2},{2,3},{3,4},{4,5},{5,6},{6,7},{8,9},{9,10},{10,11},{11... | collective-permute-start | bytes 1179656 | tf_op jit(solution)/shard_map/ppermute | solution.py:60
  14.9 27.7 %collective-permute-start.5 = (f32[289,128]{1,0:T(8,128)S(1)}, f32[289,128]{1,0:T(8,128)}, u32[]{:S(2)}, u32[]{:S(2)}) collective-permute-start(f32[289,128]{1,0:T(8,128)S(1)} %concatenate.185), channel_id=1, source_target_pairs={{0,256},{8,264},{16,272},{24,280},{32,288},{40,296},{48,304},{56,3... | collective-permute-start | bytes 443912 | tf_op jit(solution)/shard_map/cond/branch_5_fun/ppermute | solution.py:14
  46.3 2.1 %copy-start.3 = (bf16[1,2,256,128]{3,2,1,0:T(8,128)(2,1)}, bf16[1,2,256,128]{3,2,1,0:T(8,128)(2,1)S(1)}, u32[]{:S(2)}) copy-start(bf16[1,2,256,128]{3,2,1,0:T(8,128)(2,1)S(1)} %slice.376) | copy-start | bytes 393220
  47.5 1.0 copy-start.5
  51.0 1.0 copy-start.2
  58.7 7.3 %copy-start.6 = (bf16[1,2,256,128]{3,2,1,0:T(8,128)(2,1)S(1)}, bf16[1,2,256,128]{3,2,1,0:T(8,128)(2,1)}, u32[]{:S(2)}) copy-start(bf16[1,2,256,128]{3,2,1,0:T(8,128)(2,1)} %copy-done.5) | copy-start | bytes 393220
  58.7 18.5 %all-to-all-start = ((bf16[8,288,128]{2,1,0:T(8,128)(2,1)}), bf16[8,288,128]{2,1,0:T(8,128)(2,1)}, u32[]{:S(2)}, u32[]{:S(2)}) async-start(bf16[8,288,128]{2,1,0:T(8,128)(2,1)} %bitcast.32), calls=%async_computation | async-start | bytes 1179648 | tf_op jit(solution)/shard_map/all_to_all | solution.py:94
  66.3 1.6 copy-start.13
  67.2 2.9 %copy-start.4 = (bf16[1,2,256,128]{3,2,1,0:T(8,128)(2,1)S(1)}, bf16[1,2,256,128]{3,2,1,0:T(8,128)(2,1)}, u32[]{:S(2)}) copy-start(bf16[1,2,256,128]{3,2,1,0:T(8,128)(2,1)} %copy-done.3) | copy-start | bytes 393220
  78.5 21.2 %collective-permute-start.11 = (f32[288,128]{1,0:T(8,128)S(1)}, f32[288,128]{1,0:T(8,128)}, u32[]{:S(2)}, u32[]{:S(2)}) collective-permute-start(f32[288,128]{1,0:T(8,128)S(1)} %param.11), channel_id=1, source_target_pairs={{0,256},{8,264},{16,272},{24,280},{32,288},{40,296},{48,304},{56,3... | collective-permute-start | bytes 442376 | tf_op jit(solution)/shard_map/cond/branch_5_fun/ppermute | solution.py:14
  101.7 14.1 %all-to-all-start.1 = ((bf16[8,288,128]{2,1,0:T(8,128)(2,1)}), bf16[8,288,128]{2,1,0:T(8,128)(2,1)S(1)}, u32[]{:S(2)}, u32[]{:S(2)}) async-start(bf16[8,288,128]{2,1,0:T(8,128)(2,1)} %broadcast_in_dim.32), calls=%async_computation.1 | async-start | bytes 1179648 | tf_op jit(solution)/shard_map/all_to_all | solution.py:100
  105.9 1.1 copy-start.11
  105.9 1.8 %copy-start.10 = (bf16[1,2,256,128]{3,2,1,0:T(8,128)(2,1)S(1)}, bf16[1,2,256,128]{3,2,1,0:T(8,128)(2,1)}, u32[]{:S(2)}) copy-start(bf16[1,2,256,128]{3,2,1,0:T(8,128)(2,1)} %get-tuple-element.87) | copy-start | bytes 393220
  105.9 2.5 %copy-start.12 = (bf16[1,2,256,128]{3,2,1,0:T(8,128)(2,1)S(1)}, bf16[1,2,256,128]{3,2,1,0:T(8,128)(2,1)}, u32[]{:S(2)}) copy-start(bf16[1,2,256,128]{3,2,1,0:T(8,128)(2,1)} %get-tuple-element.112) | copy-start | bytes 393220
  105.9 3.2 %copy-start.9 = (bf16[1,2,256,128]{3,2,1,0:T(8,128)(2,1)S(1)}, bf16[1,2,256,128]{3,2,1,0:T(8,128)(2,1)}, u32[]{:S(2)}) copy-start(bf16[1,2,256,128]{3,2,1,0:T(8,128)(2,1)} %get-tuple-element.86) | copy-start | bytes 393220
  117.9 1.3 copy-start
  122.6 14.7 %all-to-all-start.2 = ((bf16[8,288,128]{2,1,0:T(8,128)(2,1)}), bf16[8,288,128]{2,1,0:T(8,128)(2,1)S(1)}, u32[]{:S(2)}, u32[]{:S(2)}) async-start(bf16[8,288,128]{2,1,0:T(8,128)(2,1)} %bitcast.59), calls=%async_computation.2 | async-start | bytes 1179648 | tf_op jit(solution)/shard_map/all_to_all | solution.py:94
  126.2 7.5 %collective-permute-start.12 = (f32[289,128]{1,0:T(8,128)S(1)}, f32[289,128]{1,0:T(8,128)}, u32[]{:S(2)}, u32[]{:S(2)}) collective-permute-start(f32[289,128]{1,0:T(8,128)S(1)} %concatenate.186), channel_id=1, source_target_pairs={{0,8},{8,16},{16,24},{24,32},{32,40},{40,48},{48,56},{56,64},{64,7... | collective-permute-start | bytes 443912 | tf_op jit(solution)/shard_map/cond/branch_0_fun/ppermute | solution.py:14
  137.4 7.5 %collective-permute-start.18 = (f32[288,128]{1,0:T(8,128)S(1)}, f32[288,128]{1,0:T(8,128)}, u32[]{:S(2)}, u32[]{:S(2)}) collective-permute-start(f32[288,128]{1,0:T(8,128)S(1)} %param.18), channel_id=1, source_target_pairs={{0,8},{8,16},{16,24},{24,32},{32,40},{40,48},{48,56},{56,64},{64,7... | collective-permute-start | bytes 442376 | tf_op jit(solution)/shard_map/cond/branch_0_fun/ppermute | solution.py:14
  147.0 20.8 %all-to-all-start.3 = ((f32[8,288,128]{2,1,0:T(8,128)}), f32[8,288,128]{2,1,0:T(8,128)S(1)}, u32[]{:S(2)}, u32[]{:S(2)}) async-start(f32[8,288,128]{2,1,0:T(8,128)} %broadcast_in_dim.33), calls=%async_computation.3 | async-start | bytes 2359296 | tf_op jit(solution)/shard_map/all_to_all | solution.py:100

commit v2 on v1

--- a/solution.py
+++ b/solution.py
@@ -117,7 +117,6 @@
     weight = push_weight[0]
     above, below = halo_rows(images, out_grads)
     own_rows = images.shape[3]
-    got = pushed(with_weight(sum_state, weight), step_index[0] % levels)
     for step_num in range(images.shape[0]):
         peer_level = (step_index[0] + step_num) % levels
         if step_num == 0:
@@ -126,7 +125,6 @@
             weights = gathered((sum_state / weight).astype(jnp.bfloat16), tiles).reshape(
                 kernel_shape
             )
-            got = pushed(with_weight(sum_state, weight), peer_level)
         x_ext = jnp.concatenate(
             [above[step_num][:, :own_rows], images[step_num, 0], below[step_num][:, :own_rows]],
             axis=1,
@@ -136,10 +134,9 @@
             axis=1,
         )
         grads_chunk = scattered_sum(local_grads(x_ext, g_ext, weights, first, last), tiles)
-        peer_grads = pushed(grads_chunk, peer_level)
-        own_part = sum_state - learn_rate * grads_chunk
-        peer_part = got[:state_rows] - learn_rate * peer_grads
-        sum_state = 0.5 * (own_part + peer_part)
+        sum_state = sum_state - learn_rate * grads_chunk
+        got = pushed(with_weight(sum_state, weight), peer_level)
+        sum_state = 0.5 * (sum_state + got[:state_rows])
         weight = 0.5 * (weight + got[state_rows, 0])
     new_state = gathered(sum_state, tiles).reshape(kernel_shape)
     return (new_state[None], jnp.reshape(weight, (1,)))

time: 171 us -> 176 us (1.029)
  the two profiles are of different devices: /device:TPU:32 before, /device:TPU:2 now
where the time goes in v2:
time: 176 us; the launch traced here: 175 us
  waiting for transfers between devices  72.3 us (41%)
  starting transfers between devices  52 us (30%)
  local copies, waits for them, and re-layouts  27.6 us (16%)
  other arithmetic  10.3 us (6%)
  matrix products  7.79 us (4%)
  between operations  4.98 us (3%)
    ppermute x2, starting transfers between devices, passed_along(): lax.ppermute(shard, axis, [(i, (i + by) % devices) for i in range(devices)])  28.7 us
    all_to_all x2, waiting for transfers between devices, gathered(): return lax.all_to_all(spread, 'tile', 0, 0, tiled=True)  22.6 us
    ppermute x2, waiting for transfers between devices, passed_along(): lax.ppermute(shard, axis, [(i, (i + by) % devices) for i in range(devices)])  18.5 us
    all_to_all x2, waiting for transfers between devices, scattered_sum(): got = lax.all_to_all(chunks, 'tile', 0, 0, tiled=True)  18 us
    unnamed x79, local copies, waits for them, and re-layouts  15.1 us
    ppermute x1, waiting for transfers between devices, halo_rows(): lax.ppermute(for_above, 'tile', up)  10.2 us
    all_to_all x2, starting transfers between devices, scattered_sum(): got = lax.all_to_all(chunks, 'tile', 0, 0, tiled=True)  9.41 us
    all_to_all x2, starting transfers between devices, gathered(): return lax.all_to_all(spread, 'tile', 0, 0, tiled=True)  7.85 us
  transfers between devices with their start and end apart: 8, of which 8 were waited for; matrix products, arithmetic and copies ran while one was open for 7% of the time, Pallas kernels for 0%

profile of v2, /device:TPU:2, one launch (start us, length us, event | category | flops | bytes accessed | tf_op | source)
XLA Modules:
  0.0 175.0 jit_solution(15697691456286519167)
XLA Ops:
  0.6 1.0 slice_bitcast_fusion.9
  1.7 1.8 %pad_maximum_fusion.3 = (bf16[2,1,3,256,128]{4,3,2,1,0:T(8,128)(2,1)S(1)}, bf16[2,1,3,256,128]{4,3,2,1,0:T(8,128)(2,1)}) fusion(bf16[2,1,2,256,128]{4,3,2,1,0:T(8,128)(2,1)} %bitcast.145, bf16[2,1,1,256,128]{4,3,2,1,0:T(8,128)(2,1)S(1)} %get-tuple-element.82, bf16[2,1,1,256,128]{4,3,2,1,0:T(8,128)(2,1)S(1)} %get-tuple-element.83), kind=kLoop, calls=%fused_computation.33 | loop fusion | flops 393216 | bytes 1310720 | tf_op jit(solution)/shard_map/concatenate | solution.py:56
  3.5 4.8 %collective-permute-start.12 = (bf16[2,1,3,256,128]{4,3,2,1,0:T(8,128)(2,1)S(1)}, bf16[2,1,3,256,128]{4,3,2,1,0:T(8,128)(2,1)}, u32[]{:S(2)}, u32[]{:S(2)}) collective-permute-start(bf16[2,1,3,256,128]{4,3,2,1,0:T(8,128)(2,1)S(1)} %get-tuple-element.80), channel_id=1, source_target_pairs={{0,1},{1,2},{2,3},{3,4},{4,5},{5,6},{6,7},{8,9},{9,10},{10,11},{11... | collective-permute-start | bytes 1179656 | tf_op jit(solution)/shard_map/ppermute | solution.py:60
  8.3 1.3 collective-permute-start.13
  12.9 3.0 %collective-permute-done.12 = bf16[2,1,3,256,128]{4,3,2,1,0:T(8,128)(2,1)} collective-permute-done((bf16[2,1,3,256,128]{4,3,2,1,0:T(8,128)(2,1)S(1)}, bf16[2,1,3,256,128]{4,3,2,1,0:T(8,128)(2,1)}, u32[]{:S(2)}, u32[]{:S(2)}) %collective-permute-start.12) | collective-permute-done | bytes 393248 | tf_op jit(solution)/shard_map/ppermute | solution.py:60
  15.9 1.0 slice_bitcast_fusion.5
  17.0 10.2 %collective-permute-done.13 = bf16[2,1,3,256,128]{4,3,2,1,0:T(8,128)(2,1)S(1)} collective-permute-done((bf16[2,1,3,256,128]{4,3,2,1,0:T(8,128)(2,1)}, bf16[2,1,3,256,128]{4,3,2,1,0:T(8,128)(2,1)S(1)}, u32[]{:S(2)}, u32[]{:S(2)}) %collective-permute-start.13) | collective-permute-done | bytes 393248 | tf_op jit(solution)/shard_map/ppermute | solution.py:60
  39.1 2.6 %fusion.7 = bf16[1,1152,128]{2,1,0:T(8,128)(2,1)S(1)} fusion(bf16[512,1152]{1,0:T(8,128)(2,1)S(1)} %bitcast.131, f32[512,128]{1,0:T(8,128)S(1)} %get-tuple-element.77, f32[512,128]{1,0:T(8,128)S(1)} %get-tuple-element.76, bf16[512,1152]{1,0:T(8,128)(2,1)} %constant_dynamic-update-slice_fusion, bf16[1152,128]{1,0:T(8,128)(2,1)S(1)} %bitcast.141), kind=kOutput, calls=%fused_computation.11 | convolution fusion | flops 302546944 | bytes 3473408 | tf_op jit(solution)/shard_map/dot_general | solution.py:48
  42.6 5.9 %all-to-all-start = ((bf16[8,288,128]{2,1,0:T(8,128)(2,1)}), bf16[8,288,128]{2,1,0:T(8,128)(2,1)S(1)}, u32[]{:S(2)}, u32[]{:S(2)}) async-start(bf16[8,288,128]{2,1,0:T(8,128)(2,1)} %bitcast.32), calls=%async_computation | async-start | bytes 1179648 | tf_op jit(solution)/shard_map/all_to_all | solution.py:94
  48.6 1.0 maximum_dynamic-update-slice_fusion.3
  52.4 7.5 %all-to-all-done = bf16[8,288,128]{2,1,0:T(8,128)(2,1)S(1)} async-done(((bf16[8,288,128]{2,1,0:T(8,128)(2,1)}), bf16[8,288,128]{2,1,0:T(8,128)(2,1)S(1)}, u32[]{:S(2)}, u32[]{:S(2)}) %all-to-all-start) | async-done | bytes 589856 | tf_op jit(solution)/shard_map/all_to_all | solution.py:94
  60.0 0.9 bitcast_subtract_fusion
  60.9 18.6 %conditional.2 = (f32[289,128]{1,0:T(8,128)}) conditional(s32[]{:T(128)} %clamp.6, (f32[288,128]{1,0:T(8,128)S(1)}, f32[]{:T(128)}) %tuple.45, (f32[288,128]{1,0:T(8,128)S(1)}, f32[]{:T(128)}) %tuple.45, (f32[288,128]{1,0:T(8,128)S(1)}, f32[]{:T(128)}) %tuple.45, (f32[288,128]{1,0:T(8,128)S(1)}, f32[]{:T(128)}) %tuple.45, ...), branch_computations={%region_1.2_spmd, %region_2.3_spmd, %region_3.4_spmd, %region_4.5_... | conditional | bytes 887348 | solution.py:20
  61.7 9.1 %collective-permute-start.4 = (f32[289,128]{1,0:T(8,128)S(1)}, f32[289,128]{1,0:T(8,128)}, u32[]{:S(2)}, u32[]{:S(2)}) collective-permute-start(f32[289,128]{1,0:T(8,128)S(1)} %concatenate.184), channel_id=1, source_target_pairs={{0,128},{8,136},{16,144},{24,152},{32,160},{40,168},{48,176},{56,1... | collective-permute-start | bytes 443912 | tf_op jit(solution)/shard_map/cond/branch_4_fun/ppermute | solution.py:14
  70.8 8.8 %collective-permute-done.4 = f32[289,128]{1,0:T(8,128)} collective-permute-done((f32[289,128]{1,0:T(8,128)S(1)}, f32[289,128]{1,0:T(8,128)}, u32[]{:S(2)}, u32[]{:S(2)}) %collective-permute-start.4) | collective-permute-done | bytes 148000 | tf_op jit(solution)/shard_map/cond/branch_4_fun/ppermute | solution.py:14
  79.5 1.2 slice.387
  81.4 0.9 divide_convert_fusion.1
  83.3 3.5 %all-to-all-start.1 = ((bf16[8,288,128]{2,1,0:T(8,128)(2,1)}), bf16[8,288,128]{2,1,0:T(8,128)(2,1)S(1)}, u32[]{:S(2)}, u32[]{:S(2)}) async-start(bf16[8,288,128]{2,1,0:T(8,128)(2,1)} %broadcast_in_dim.32), calls=%async_computation.1 | async-start | bytes 1179648 | tf_op jit(solution)/shard_map/all_to_all | solution.py:100
  87.5 1.1 slice.378
  91.3 5.9 %all-to-all-done.1 = bf16[8,288,128]{2,1,0:T(8,128)(2,1)S(1)} async-done(((bf16[8,288,128]{2,1,0:T(8,128)(2,1)}), bf16[8,288,128]{2,1,0:T(8,128)(2,1)S(1)}, u32[]{:S(2)}, u32[]{:S(2)}) %all-to-all-start.1) | async-done | bytes 589856 | tf_op jit(solution)/shard_map/all_to_all | solution.py:100
  100.3 2.6 %fusion.5 = bf16[1,1152,128]{2,1,0:T(8,128)(2,1)S(1)} fusion(bf16[512,1152]{1,0:T(8,128)(2,1)S(1)} %bitcast.130, f32[512,128]{1,0:T(8,128)S(1)} %get-tuple-element.75, f32[512,128]{1,0:T(8,128)S(1)} %get-tuple-element.74, bf16[512,1152]{1,0:T(8,128)(2,1)} %constant_dynamic-update-slice_fusion.9, bf16[1152,128]{1,0:T(8,128)(2,1)S(1)} %bitcast.142), kind=kOutput, calls=%fused_computation.9 | convolution fusion | flops 302546944 | bytes 3473408 | tf_op jit(solution)/shard_map/dot_general | solution.py:48
  103.7 3.5 %all-to-all-start.2 = ((bf16[8,288,128]{2,1,0:T(8,128)(2,1)}), bf16[8,288,128]{2,1,0:T(8,128)(2,1)S(1)}, u32[]{:S(2)}, u32[]{:S(2)}) async-start(bf16[8,288,128]{2,1,0:T(8,128)(2,1)} %bitcast.59), calls=%async_computation.2 | async-start | bytes 1179648 | tf_op jit(solution)/shard_map/all_to_all | solution.py:94
  107.3 10.5 %all-to-all-done.2 = bf16[8,288,128]{2,1,0:T(8,128)(2,1)S(1)} async-done(((bf16[8,288,128]{2,1,0:T(8,128)(2,1)}), bf16[8,288,128]{2,1,0:T(8,128)(2,1)S(1)}, u32[]{:S(2)}, u32[]{:S(2)}) %all-to-all-start.2) | async-done | bytes 589856 | tf_op jit(solution)/shard_map/all_to_all | solution.py:94
  117.8 1.0 multiply_subtract_fusion
  118.8 29.4 %conditional.3 = (f32[289,128]{1,0:T(8,128)}) conditional(s32[]{:T(128)} %clamp.7, (f32[288,128]{1,0:T(8,128)S(1)}, f32[]{:T(128)}) %tuple.46, (f32[288,128]{1,0:T(8,128)S(1)}, f32[]{:T(128)}) %tuple.46, (f32[288,128]{1,0:T(8,128)S(1)}, f32[]{:T(128)}) %tuple.46, (f32[288,128]{1,0:T(8,128)S(1)}, f32[]{:T(128)}) %tuple.46, ...), branch_computations={%region_8.9_spmd, %region_9.10_spmd, %region_10.11_spmd, %region_1... | conditional | bytes 887348 | solution.py:20
  118.9 19.6 %collective-permute-start.11 = (f32[289,128]{1,0:T(8,128)S(1)}, f32[289,128]{1,0:T(8,128)}, u32[]{:S(2)}, u32[]{:S(2)}) collective-permute-start(f32[289,128]{1,0:T(8,128)S(1)} %concatenate.191), channel_id=1, source_target_pairs={{0,256},{8,264},{16,272},{24,280},{32,288},{40,296},{48,304},{56,3... | collective-permute-start | bytes 443912 | tf_op jit(solution)/shard_map/cond/branch_5_fun/ppermute | solution.py:14
  138.4 9.7 %collective-permute-done.11 = f32[289,128]{1,0:T(8,128)} collective-permute-done((f32[289,128]{1,0:T(8,128)S(1)}, f32[289,128]{1,0:T(8,128)}, u32[]{:S(2)}, u32[]{:S(2)}) %collective-permute-start.11) | collective-permute-done | bytes 148000 | tf_op jit(solution)/shard_map/cond/branch_5_fun/ppermute | solution.py:14
  149.1 1.1 broadcast_in_dim.33
  150.2 4.3 %all-to-all-start.3 = ((f32[8,288,128]{2,1,0:T(8,128)}), f32[8,288,128]{2,1,0:T(8,128)S(1)}, u32[]{:S(2)}, u32[]{:S(2)}) async-start(f32[8,288,128]{2,1,0:T(8,128)} %broadcast_in_dim.33), calls=%async_computation.3 | async-start | bytes 2359296 | tf_op jit(solution)/shard_map/all_to_all | solution.py:100
  154.5 1.2 slice.395
  156.3 16.6 %all-to-all-done.3 = f32[8,288,128]{2,1,0:T(8,128)S(1)} async-done(((f32[8,288,128]{2,1,0:T(8,128)}), f32[8,288,128]{2,1,0:T(8,128)S(1)}, u32[]{:S(2)}, u32[]{:S(2)}) %all-to-all-start.3) | async-done | bytes 1179680 | tf_op jit(solution)/shard_map/all_to_all | solution.py:100
  172.9 1.0 copy.78
  (130 shorter events, 27.1 us)
Async XLA Ops:
  0.6 9.0 %copy-start.8 = (bf16[2,1,1,2,256,128]{5,4,3,2,1,0:T(8,128)(2,1)S(1)}, bf16[2,1,1,2,256,128]{5,4,3,2,1,0:T(8,128)(2,1)}, u32[]{:S(2)}) copy-start(bf16[2,1,1,2,256,128]{5,4,3,2,1,0:T(8,128)(2,1)} %param.18) | copy-start | bytes 786436
  1.7 9.3 %copy-start.3 = (f32[1,2,1152,128]{3,2,1,0:T(8,128)S(1)}, f32[1,2,1152,128]{3,2,1,0:T(8,128)}, u32[]{:S(2)}) copy-start(f32[1,2,1152,128]{3,2,1,0:T(8,128)} %param.19) | copy-start | bytes 3538948
  3.5 12.4 %collective-permute-start.12 = (bf16[2,1,3,256,128]{4,3,2,1,0:T(8,128)(2,1)S(1)}, bf16[2,1,3,256,128]{4,3,2,1,0:T(8,128)(2,1)}, u32[]{:S(2)}, u32[]{:S(2)}) collective-permute-start(bf16[2,1,3,256,128]{4,3,2,1,0:T(8,128)(2,1)S(1)} %get-tuple-element.80), channel_id=1, source_target_pairs={{0,1},{1,2},{2,3},{3,4},{4,5},{5,6},{6,7},{8,9},{9,10},{10,11},{11... | collective-permute-start | bytes 1179656 | tf_op jit(solution)/shard_map/ppermute | solution.py:60
  8.3 18.9 %collective-permute-start.13 = (bf16[2,1,3,256,128]{4,3,2,1,0:T(8,128)(2,1)}, bf16[2,1,3,256,128]{4,3,2,1,0:T(8,128)(2,1)S(1)}, u32[]{:S(2)}, u32[]{:S(2)}) collective-permute-start(bf16[2,1,3,256,128]{4,3,2,1,0:T(8,128)(2,1)} %get-tuple-element.81), channel_id=1, source_target_pairs={{1,0},{2,1},{3,2},{4,3},{5,4},{6,5},{7,6},{9,8},{10,9},{11,10},{12... | collective-permute-start | bytes 1179656 | tf_op jit(solution)/shard_map/ppermute | solution.py:60
  11.0 1.0 copy-start.9
  12.0 18.7 %copy-start.1 = (bf16[1,2,256,128]{3,2,1,0:T(8,128)(2,1)}, bf16[1,2,256,128]{3,2,1,0:T(8,128)(2,1)S(1)}, u32[]{:S(2)}) copy-start(bf16[1,2,256,128]{3,2,1,0:T(8,128)(2,1)S(1)} %get-tuple-element.79) | copy-start | bytes 393220
  28.3 2.8 %copy-start.7 = (bf16[1,2,256,128]{3,2,1,0:T(8,128)(2,1)}, bf16[1,2,256,128]{3,2,1,0:T(8,128)(2,1)S(1)}, u32[]{:S(2)}) copy-start(bf16[1,2,256,128]{3,2,1,0:T(8,128)(2,1)S(1)} %slice.374) | copy-start | bytes 393220
  28.3 2.4 %copy-start.5 = (bf16[1,2,256,128]{3,2,1,0:T(8,128)(2,1)}, bf16[1,2,256,128]{3,2,1,0:T(8,128)(2,1)S(1)}, u32[]{:S(2)}) copy-start(bf16[1,2,256,128]{3,2,1,0:T(8,128)(2,1)S(1)} %slice.376) | copy-start | bytes 393220
  42.6 5.9 %copy-start.2 = (bf16[1,2,256,128]{3,2,1,0:T(8,128)(2,1)S(1)}, bf16[1,2,256,128]{3,2,1,0:T(8,128)(2,1)}, u32[]{:S(2)}) copy-start(bf16[1,2,256,128]{3,2,1,0:T(8,128)(2,1)} %copy-done.1) | copy-start | bytes 393220
  42.6 17.3 %all-to-all-start = ((bf16[8,288,128]{2,1,0:T(8,128)(2,1)}), bf16[8,288,128]{2,1,0:T(8,128)(2,1)S(1)}, u32[]{:S(2)}, u32[]{:S(2)}) async-start(bf16[8,288,128]{2,1,0:T(8,128)(2,1)} %bitcast.32), calls=%async_computation | async-start | bytes 1179648 | tf_op jit(solution)/shard_map/all_to_all | solution.py:94
  48.5 1.3 copy-start.16
  49.6 1.0 copy-start.14
  49.6 1.7 copy-start.13
  49.9 2.3 %copy-start.6 = (bf16[1,2,256,128]{3,2,1,0:T(8,128)(2,1)S(1)}, bf16[1,2,256,128]{3,2,1,0:T(8,128)(2,1)}, u32[]{:S(2)}) copy-start(bf16[1,2,256,128]{3,2,1,0:T(8,128)(2,1)} %copy-done.5) | copy-start | bytes 393220
  61.7 17.9 %collective-permute-start.4 = (f32[289,128]{1,0:T(8,128)S(1)}, f32[289,128]{1,0:T(8,128)}, u32[]{:S(2)}, u32[]{:S(2)}) collective-permute-start(f32[289,128]{1,0:T(8,128)S(1)} %concatenate.184), channel_id=1, source_target_pairs={{0,128},{8,136},{16,144},{24,152},{32,160},{40,168},{48,176},{56,1... | collective-permute-start | bytes 443912 | tf_op jit(solution)/shard_map/cond/branch_4_fun/ppermute | solution.py:14
  79.5 7.3 %copy-start.4 = (bf16[1,1,1,2,256,128]{5,4,3,2,1,0:T(8,128)(2,1)S(1)}, bf16[1,1,1,2,256,128]{5,4,3,2,1,0:T(8,128)(2,1)}, u32[]{:S(2)}) copy-start(bf16[1,1,1,2,256,128]{5,4,3,2,1,0:T(8,128)(2,1)} %get-tuple-element.72) | copy-start | bytes 393220
  83.3 14.0 %all-to-all-start.1 = ((bf16[8,288,128]{2,1,0:T(8,128)(2,1)}), bf16[8,288,128]{2,1,0:T(8,128)(2,1)S(1)}, u32[]{:S(2)}, u32[]{:S(2)}) async-start(bf16[8,288,128]{2,1,0:T(8,128)(2,1)} %broadcast_in_dim.32), calls=%async_computation.1 | async-start | bytes 1179648 | tf_op jit(solution)/shard_map/all_to_all | solution.py:100
  87.5 1.1 copy-start.12
  87.5 1.8 %copy-start.11 = (bf16[1,2,256,128]{3,2,1,0:T(8,128)(2,1)S(1)}, bf16[1,2,256,128]{3,2,1,0:T(8,128)(2,1)}, u32[]{:S(2)}) copy-start(bf16[1,2,256,128]{3,2,1,0:T(8,128)(2,1)} %get-tuple-element.59) | copy-start | bytes 393220
  87.5 2.5 %copy-start.15 = (bf16[1,2,256,128]{3,2,1,0:T(8,128)(2,1)S(1)}, bf16[1,2,256,128]{3,2,1,0:T(8,128)(2,1)}, u32[]{:S(2)}) copy-start(bf16[1,2,256,128]{3,2,1,0:T(8,128)(2,1)} %get-tuple-element.84) | copy-start | bytes 393220
  87.5 3.2 %copy-start.10 = (bf16[1,2,256,128]{3,2,1,0:T(8,128)(2,1)S(1)}, bf16[1,2,256,128]{3,2,1,0:T(8,128)(2,1)}, u32[]{:S(2)}) copy-start(bf16[1,2,256,128]{3,2,1,0:T(8,128)(2,1)} %get-tuple-element.58) | copy-start | bytes 393220
  99.0 1.3 copy-start
  103.7 14.0 %all-to-all-start.2 = ((bf16[8,288,128]{2,1,0:T(8,128)(2,1)}), bf16[8,288,128]{2,1,0:T(8,128)(2,1)S(1)}, u32[]{:S(2)}, u32[]{:S(2)}) async-start(bf16[8,288,128]{2,1,0:T(8,128)(2,1)} %bitcast.59), calls=%async_computation.2 | async-start | bytes 1179648 | tf_op jit(solution)/shard_map/all_to_all | solution.py:94
  118.9 29.3 %collective-permute-start.11 = (f32[289,128]{1,0:T(8,128)S(1)}, f32[289,128]{1,0:T(8,128)}, u32[]{:S(2)}, u32[]{:S(2)}) collective-permute-start(f32[289,128]{1,0:T(8,128)S(1)} %concatenate.191), channel_id=1, source_target_pairs={{0,256},{8,264},{16,272},{24,280},{32,288},{40,296},{48,304},{56,3... | collective-permute-start | bytes 443912 | tf_op jit(solution)/shard_map/cond/branch_5_fun/ppermute | solution.py:14
  150.2 22.7 %all-to-all-start.3 = ((f32[8,288,128]{2,1,0:T(8,128)}), f32[8,288,128]{2,1,0:T(8,128)S(1)}, u32[]{:S(2)}, u32[]{:S(2)}) async-start(f32[8,288,128]{2,1,0:T(8,128)} %broadcast_in_dim.33), calls=%async_computation.3 | async-start | bytes 2359296 | tf_op jit(solution)/shard_map/all_to_all | solution.py:100

commit v3 on v2

--- a/solution.py
+++ b/solution.py
@@ -20,19 +20,16 @@
     return lax.switch(level, branches, payload)
 
 
-def pad_columns(field_in):
-    return jnp.pad(field_in, ((0, 0), (0, 0), (1, 1), (0, 0)))
-
-
-def patches(padded):
-    out_rows = padded.shape[1] - 2
-    out_cols = padded.shape[2] - 2
-    pieces = [
-        padded[:, row_off : row_off + out_rows, col_off : col_off + out_cols, :]
-        for row_off in range(3)
-        for col_off in range(3)
-    ]
-    return jnp.concatenate(pieces, axis=-1).reshape(-1, 9 * padded.shape[3])
+def conv_rows(field, kernel):
+    channels = kernel.shape[1]
+    return lax.conv_general_dilated(
+        field,
+        kernel.reshape(3, 3, channels, channels),
+        (1, 1),
+        ((0, 0), (1, 1)),
+        dimension_numbers=("NHWC", "HWIO", "NHWC"),
+        preferred_element_type=jnp.float32,
+    )
 
 
 def flipped(kernel):
@@ -44,10 +41,17 @@
     )
 
 
-def contract_rows(left_mat, right_mat):
-    return lax.dot_general(
-        left_mat, right_mat, (((0,), (0,)), ((), ())), preferred_element_type=jnp.float32
+def kernel_grad(field, cotangent):
+    padded = jnp.pad(field, ((0, 0), (0, 0), (1, 1), (0, 0)))
+    out = lax.conv_general_dilated(
+        padded,
+        cotangent,
+        (1, 1),
+        "VALID",
+        dimension_numbers=("CHWN", "IHWO", "NHWC"),
+        preferred_element_type=jnp.float32,
     )
+    return out.transpose(1, 2, 0, 3).reshape(-1, cotangent.shape[-1])
 
 
 def halo_rows(images, out_grads):
@@ -61,31 +65,22 @@
 
 
 def local_grads(x_ext, g_ext, weights, first, last):
-    batch_size, ext_rows, columns, channels = x_ext.shape
-    own_rows = ext_rows - 4
+    channels = x_ext.shape[-1]
+    own_rows = x_ext.shape[1] - 4
     norm_scale = 1.0 / math.sqrt(9 * channels)
-    input_patches = patches(pad_columns(x_ext))
-    pre_ext = norm_scale * jnp.dot(input_patches, weights[0], preferred_element_type=jnp.float32)
-    pre_ext = pre_ext.reshape(batch_size, own_rows + 2, columns, channels)
+    pre_ext = norm_scale * conv_rows(x_ext, weights[0])
     row_ids = lax.broadcasted_iota(jnp.int32, (1, own_rows + 2, 1, 1), 1)
     outside = ((row_ids == 0) & first) | ((row_ids == own_rows + 1) & last)
     hidden_ext = jnp.where(outside, 0.0, jax.nn.silu(pre_ext)).astype(jnp.bfloat16)
-    pre_act = pre_ext[:, 1 : own_rows + 1].reshape(-1, channels)
-    own_input_patches = input_patches.reshape(batch_size, own_rows + 2, columns, -1)[
-        :, 1 : own_rows + 1
-    ].reshape(-1, 9 * channels)
-    hidden_patches = patches(pad_columns(hidden_ext))
-    grad_patches = patches(pad_columns(g_ext))
-    grad_hidden = norm_scale * jnp.dot(
-        grad_patches, flipped(weights[1]), preferred_element_type=jnp.float32
-    )
+    pre_act = pre_ext[:, 1 : own_rows + 1]
+    grad_hidden = norm_scale * conv_rows(g_ext, flipped(weights[1]))
     sigmoid_val = jax.nn.sigmoid(pre_act)
     grad_pre = (grad_hidden * sigmoid_val * (1.0 + pre_act * (1.0 - sigmoid_val))).astype(
         jnp.bfloat16
     )
-    grad_own = g_ext[:, 1 : own_rows + 1].reshape(-1, channels)
-    first_grad = norm_scale * contract_rows(own_input_patches, grad_pre)
-    second = norm_scale * contract_rows(hidden_patches, grad_own)
+    grad_own = g_ext[:, 1 : own_rows + 1]
+    first_grad = norm_scale * kernel_grad(x_ext[:, 1 : own_rows + 3], grad_pre)
+    second = norm_scale * kernel_grad(hidden_ext, grad_own)
     return jnp.stack([first_grad, second])
 
 

time: 176 us -> 170 us (0.966)
  local copies, waits for them, and re-layouts: 27.6 us -> 18.4 us
  waiting for transfers between devices: 72.3 us -> 78.7 us
  other arithmetic: 10.3 us -> 7.13 us
    unnamed x79 -> x39, local copies, waits for them, and re-layouts: 15.1 us -> 6.08 us
    dot_general x6 -> x0, matrix products: 7.79 us -> none  [the longest x4 6.22 us: contract_rows(): lax.dot_general(left_mat, right_mat, (((0,), (0,)), ((), ())), preferred_...]
    transpose x0 -> x4, matrix products: none -> 5.08 us  [kernel_grad(): return out.transpose(1, 2, 0, 3).reshape(-1, cotangent.shape[-1])]
    conv_general_dilated x0 -> x2, matrix products: none -> 3.44 us  [conv_rows(): lax.conv_general_dilated(field, kernel.reshape(3, 3, channels, channels),...]
    all_to_all x2, waiting for transfers between devices: 22.6 us -> 24.6 us  [gathered(): return lax.all_to_all(spread, 'tile', 0, 0, tiled=True)]
    all_to_all x2, waiting for transfers between devices: 18 us -> 20 us  [scattered_sum(): got = lax.all_to_all(chunks, 'tile', 0, 0, tiled=True)]
  transfers between devices with their start and end apart: 8 -> 8, of which waited for: 8 -> 8; matrix products, arithmetic and copies ran while one was open for 7% -> 3% of each run, Pallas kernels for 0% -> 0%
where the time goes in v3:
time: 170 us; the launch traced here: 169 us
  waiting for transfers between devices  78.7 us (46%)
  starting transfers between devices  51.3 us (30%)
  local copies, waits for them, and re-layouts  18.4 us (11%)
  matrix products  8.52 us (5%)
  other arithmetic  7.13 us (4%)
  between operations  4.99 us (3%)
    ppermute x2, starting transfers between devices, passed_along(): lax.ppermute(shard, axis, [(i, (i + by) % devices) for i in range(devices)])  28.6 us
    all_to_all x2, waiting for transfers between devices, gathered(): return lax.all_to_all(spread, 'tile', 0, 0, tiled=True)  24.6 us
    all_to_all x2, waiting for transfers between devices, scattered_sum(): got = lax.all_to_all(chunks, 'tile', 0, 0, tiled=True)  20 us
    ppermute x2, waiting for transfers between devices, passed_along(): lax.ppermute(shard, axis, [(i, (i + by) % devices) for i in range(devices)])  18.5 us
    ppermute x1, waiting for transfers between devices, halo_rows(): lax.ppermute(for_above, 'tile', up)  11.2 us
    all_to_all x2, starting transfers between devices, scattered_sum(): got = lax.all_to_all(chunks, 'tile', 0, 0, tiled=True)  9.27 us
    all_to_all x2, starting transfers between devices, gathered(): return lax.all_to_all(spread, 'tile', 0, 0, tiled=True)  8.04 us
    unnamed x39, local copies, waits for them, and re-layouts  6.08 us
  transfers between devices with their start and end apart: 8, of which 8 were waited for; matrix products, arithmetic and copies ran while one was open for 3% of the time, Pallas kernels for 0%

profile of v3, /device:TPU:2, one launch (start us, length us, event | category | flops | bytes accessed | tf_op | source)
XLA Modules:
  0.0 169.2 jit_solution(11298738721650646285)
XLA Ops:
  0.6 1.1 slice_bitcast_fusion.7
  1.7 1.0 pad_maximum_fusion.5
  2.7 4.1 %collective-permute-start.12 = (bf16[2,1,3,256,128]{4,3,2,1,0:T(8,128)(2,1)S(1)}, bf16[2,1,3,256,128]{4,3,2,1,0:T(8,128)(2,1)S(1)}, u32[]{:S(2)}, u32[]{:S(2)}) collective-permute-start(bf16[2,1,3,256,128]{4,3,2,1,0:T(8,128)(2,1)S(1)} %get-tuple-element.86), channel_id=1, source_target_pairs={{0,1},{1,2},{2,3},{3,4},{4,5},{5,6},{6,7},{8,9},{9,10},{10,11},{11... | collective-permute-start | bytes 1179656 | tf_op jit(solution)/shard_map/ppermute | solution.py:64
  6.8 1.3 collective-permute-start.13
  10.8 4.3 %collective-permute-done.12 = bf16[2,1,3,256,128]{4,3,2,1,0:T(8,128)(2,1)S(1)} collective-permute-done((bf16[2,1,3,256,128]{4,3,2,1,0:T(8,128)(2,1)S(1)}, bf16[2,1,3,256,128]{4,3,2,1,0:T(8,128)(2,1)S(1)}, u32[]{:S(2)}, u32[]{:S(2)}) %collective-permute-start.12) | collective-permute-done | bytes 393248 | tf_op jit(solution)/shard_map/ppermute | solution.py:64
  15.2 11.2 %collective-permute-done.13 = bf16[2,1,3,256,128]{4,3,2,1,0:T(8,128)(2,1)S(1)} collective-permute-done((bf16[2,1,3,256,128]{4,3,2,1,0:T(8,128)(2,1)S(1)}, bf16[2,1,3,256,128]{4,3,2,1,0:T(8,128)(2,1)S(1)}, u32[]{:S(2)}, u32[]{:S(2)}) %collective-permute-start.13) | collective-permute-done | bytes 393248 | tf_op jit(solution)/shard_map/ppermute | solution.py:64
  29.5 1.7 %fusion.110 = (bf16[4,8,33,128]{3,1,2,0:T(8,128)(2,1)S(1)}, f32[4,8,33,128]{3,1,2,0:T(8,128)}) fusion(pred[4]{0:T(512)(128)(4,1)S(1)} %and_or_fusion, pred[8,33]{0,1:T(8,128)(4,1)S(1)} %copy-done.11, bf16[3,3,128,128]{3,2,1,0:T(8,128)(2,1)S(1)} %bitcast.153, bf16[6,1,7,2,128]{4,2,3,0,1:T(8,128)(2,1)S(1)} %slice.156, bf16[6,1,8,33,128]{4,2,3,0,1:T(8,128)(2,1)S(1)} %copy.26), kind=kOutput, calls=%fused_computation.121 | convolution fusion | flops 313933824 | bytes 1533196 | tf_op jit(solution)/shard_map/conv_general_dilated | solution.py:25
  34.1 2.3 %fusion.12 = bf16[3,3,128,128,1]{3,2,1,4,0:T(8,128)(2,1)S(1)} fusion(bf16[6,8,33,128,1]{3,1,4,2,0:T(8,128)(2,1)S(1)} %fusion.63, bf16[6,8,33,128,1]{3,1,4,2,0:T(8,128)(2,1)S(1)} %copy.21, bf16[6,8,33,128,1]{3,1,4,2,0:T(8,128)(2,1)S(1)} %fusion.59, bf16[3,3,128,128]{3,2,1,0:T(8,128)(2,1)S(1)} %bitcast.152, bf16[4,1,7,2,128]{4,2,3,0,1:T(8,128)(2,1)S(1)} %slice.154, ...), kind=kOutput, calls=%fused_computation.18 | convolution fusion | flops 317042688 | bytes 2361608 | tf_op jit(solution)/shard_map/transpose | solution.py:54
  37.3 5.7 %all-to-all-start = ((bf16[8,288,128]{2,1,0:T(8,128)(2,1)}), bf16[8,288,128]{2,1,0:T(8,128)(2,1)S(1)}, u32[]{:S(2)}, u32[]{:S(2)}) async-start(bf16[8,288,128]{2,1,0:T(8,128)(2,1)} %bitcast.31), calls=%async_computation | async-start | bytes 1179648 | tf_op jit(solution)/shard_map/all_to_all | solution.py:89
  45.0 9.6 %all-to-all-done = bf16[8,288,128]{2,1,0:T(8,128)(2,1)S(1)} async-done(((bf16[8,288,128]{2,1,0:T(8,128)(2,1)}), bf16[8,288,128]{2,1,0:T(8,128)(2,1)S(1)}, u32[]{:S(2)}, u32[]{:S(2)}) %all-to-all-start) | async-done | bytes 589856 | tf_op jit(solution)/shard_map/all_to_all | solution.py:89
  54.6 0.9 bitcast_subtract_fusion
  55.6 18.6 %conditional.2 = (f32[289,128]{1,0:T(8,128)}) conditional(s32[]{:T(128)} %clamp.6, (f32[288,128]{1,0:T(8,128)S(1)}, f32[]{:T(128)}) %tuple.45, (f32[288,128]{1,0:T(8,128)S(1)}, f32[]{:T(128)}) %tuple.45, (f32[288,128]{1,0:T(8,128)S(1)}, f32[]{:T(128)}) %tuple.45, (f32[288,128]{1,0:T(8,128)S(1)}, f32[]{:T(128)}) %tuple.45, ...), branch_computations={%region_1.2_spmd, %region_2.3_spmd, %region_3.4_spmd, %region_4.5_... | conditional | bytes 887348 | solution.py:20
  56.3 9.1 %collective-permute-start.4 = (f32[289,128]{1,0:T(8,128)S(1)}, f32[289,128]{1,0:T(8,128)}, u32[]{:S(2)}, u32[]{:S(2)}) collective-permute-start(f32[289,128]{1,0:T(8,128)S(1)} %concatenate.72), channel_id=1, source_target_pairs={{0,128},{8,136},{16,144},{24,152},{32,160},{40,168},{48,176},{56,1... | collective-permute-start | bytes 443912 | tf_op jit(solution)/shard_map/cond/branch_4_fun/ppermute | solution.py:14
  65.4 8.8 %collective-permute-done.4 = f32[289,128]{1,0:T(8,128)} collective-permute-done((f32[289,128]{1,0:T(8,128)S(1)}, f32[289,128]{1,0:T(8,128)}, u32[]{:S(2)}, u32[]{:S(2)}) %collective-permute-start.4) | collective-permute-done | bytes 148000 | tf_op jit(solution)/shard_map/cond/branch_4_fun/ppermute | solution.py:14
  74.1 1.2 slice.175
  76.0 0.9 divide_convert_fusion.1
  77.8 3.7 %all-to-all-start.1 = ((bf16[8,288,128]{2,1,0:T(8,128)(2,1)}), bf16[8,288,128]{2,1,0:T(8,128)(2,1)S(1)}, u32[]{:S(2)}, u32[]{:S(2)}) async-start(bf16[8,288,128]{2,1,0:T(8,128)(2,1)} %broadcast_in_dim.32), calls=%async_computation.1 | async-start | bytes 1179648 | tf_op jit(solution)/shard_map/all_to_all | solution.py:95
  83.7 8.1 %all-to-all-done.1 = bf16[8,288,128]{2,1,0:T(8,128)(2,1)S(1)} async-done(((bf16[8,288,128]{2,1,0:T(8,128)(2,1)}), bf16[8,288,128]{2,1,0:T(8,128)(2,1)S(1)}, u32[]{:S(2)}, u32[]{:S(2)}) %all-to-all-start.1) | async-done | bytes 589856 | tf_op jit(solution)/shard_map/all_to_all | solution.py:95
  91.9 1.7 %fusion.111 = (bf16[4,8,33,128]{3,1,2,0:T(8,128)(2,1)S(1)}, f32[4,8,33,128]{3,1,2,0:T(8,128)}) fusion(pred[4]{0:T(512)(128)(4,1)S(1)} %and_or_fusion, pred[8,33]{0,1:T(8,128)(4,1)S(1)} %copy-done.11, bf16[3,3,128,128]{3,2,1,0:T(8,128)(2,1)S(1)} %bitcast.159, bf16[6,1,7,2,128]{4,2,3,0,1:T(8,128)(2,1)S(1)} %slice.177, bf16[6,1,8,33,128]{4,2,3,0,1:T(8,128)(2,1)S(1)} %copy.40), kind=kOutput, calls=%fused_computation.122 | convolution fusion | flops 313933824 | bytes 1533196 | tf_op jit(solution)/shard_map/conv_general_dilated | solution.py:25
  95.7 1.4 fusion.15
  97.9 3.5 %all-to-all-start.2 = ((bf16[8,288,128]{2,1,0:T(8,128)(2,1)}), bf16[8,288,128]{2,1,0:T(8,128)(2,1)S(1)}, u32[]{:S(2)}, u32[]{:S(2)}) async-start(bf16[8,288,128]{2,1,0:T(8,128)(2,1)} %bitcast.57), calls=%async_computation.2 | async-start | bytes 1179648 | tf_op jit(solution)/shard_map/all_to_all | solution.py:89
  101.5 10.5 %all-to-all-done.2 = bf16[8,288,128]{2,1,0:T(8,128)(2,1)S(1)} async-done(((bf16[8,288,128]{2,1,0:T(8,128)(2,1)}), bf16[8,288,128]{2,1,0:T(8,128)(2,1)S(1)}, u32[]{:S(2)}, u32[]{:S(2)}) %all-to-all-start.2) | async-done | bytes 589856 | tf_op jit(solution)/shard_map/all_to_all | solution.py:89
  112.0 1.0 multiply_subtract_fusion
  113.0 29.3 %conditional.3 = (f32[289,128]{1,0:T(8,128)}) conditional(s32[]{:T(128)} %clamp.7, (f32[288,128]{1,0:T(8,128)S(1)}, f32[]{:T(128)}) %tuple.46, (f32[288,128]{1,0:T(8,128)S(1)}, f32[]{:T(128)}) %tuple.46, (f32[288,128]{1,0:T(8,128)S(1)}, f32[]{:T(128)}) %tuple.46, (f32[288,128]{1,0:T(8,128)S(1)}, f32[]{:T(128)}) %tuple.46, ...), branch_computations={%region_8.9_spmd, %region_9.10_spmd, %region_10.11_spmd, %region_1... | conditional | bytes 887348 | solution.py:20
  113.0 19.5 %collective-permute-start.11 = (f32[289,128]{1,0:T(8,128)S(1)}, f32[289,128]{1,0:T(8,128)}, u32[]{:S(2)}, u32[]{:S(2)}) collective-permute-start(f32[289,128]{1,0:T(8,128)S(1)} %concatenate.79), channel_id=1, source_target_pairs={{0,256},{8,264},{16,272},{24,280},{32,288},{40,296},{48,304},{56,3... | collective-permute-start | bytes 443912 | tf_op jit(solution)/shard_map/cond/branch_5_fun/ppermute | solution.py:14
  132.6 9.7 %collective-permute-done.11 = f32[289,128]{1,0:T(8,128)} collective-permute-done((f32[289,128]{1,0:T(8,128)S(1)}, f32[289,128]{1,0:T(8,128)}, u32[]{:S(2)}, u32[]{:S(2)}) %collective-permute-start.11) | collective-permute-done | bytes 148000 | tf_op jit(solution)/shard_map/cond/branch_5_fun/ppermute | solution.py:14
  142.3 0.9 fusion.114
  143.2 1.1 broadcast_in_dim.33
  144.3 4.3 %all-to-all-start.3 = ((f32[8,288,128]{2,1,0:T(8,128)}), f32[8,288,128]{2,1,0:T(8,128)S(1)}, u32[]{:S(2)}, u32[]{:S(2)}) async-start(f32[8,288,128]{2,1,0:T(8,128)} %broadcast_in_dim.33), calls=%async_computation.3 | async-start | bytes 2359296 | tf_op jit(solution)/shard_map/all_to_all | solution.py:95
  148.6 1.2 slice.185
  150.5 16.5 %all-to-all-done.3 = f32[8,288,128]{2,1,0:T(8,128)S(1)} async-done(((f32[8,288,128]{2,1,0:T(8,128)}), f32[8,288,128]{2,1,0:T(8,128)S(1)}, u32[]{:S(2)}, u32[]{:S(2)}) %all-to-all-start.3) | async-done | bytes 1179680 | tf_op jit(solution)/shard_map/all_to_all | solution.py:95
  167.0 1.0 copy.80
  (103 shorter events, 16.6 us)
Async XLA Ops:
  0.6 8.1 %copy-start = (f32[1,2,1152,128]{3,2,1,0:T(8,128)S(1)}, f32[1,2,1152,128]{3,2,1,0:T(8,128)}, u32[]{:S(2)}) copy-start(f32[1,2,1152,128]{3,2,1,0:T(8,128)} %param.19) | copy-start | bytes 3538948
  2.7 12.4 %collective-permute-start.12 = (bf16[2,1,3,256,128]{4,3,2,1,0:T(8,128)(2,1)S(1)}, bf16[2,1,3,256,128]{4,3,2,1,0:T(8,128)(2,1)S(1)}, u32[]{:S(2)}, u32[]{:S(2)}) collective-permute-start(bf16[2,1,3,256,128]{4,3,2,1,0:T(8,128)(2,1)S(1)} %get-tuple-element.86), channel_id=1, source_target_pairs={{0,1},{1,2},{2,3},{3,4},{4,5},{5,6},{6,7},{8,9},{9,10},{10,11},{11... | collective-permute-start | bytes 1179656 | tf_op jit(solution)/shard_map/ppermute | solution.py:64
  6.8 19.6 %collective-permute-start.13 = (bf16[2,1,3,256,128]{4,3,2,1,0:T(8,128)(2,1)S(1)}, bf16[2,1,3,256,128]{4,3,2,1,0:T(8,128)(2,1)S(1)}, u32[]{:S(2)}, u32[]{:S(2)}) collective-permute-start(bf16[2,1,3,256,128]{4,3,2,1,0:T(8,128)(2,1)S(1)} %get-tuple-element.87), channel_id=1, source_target_pairs={{1,0},{2,1},{3,2},{4,3},{5,4},{6,5},{7,6},{9,8},{10,9},{11,10},{12... | collective-permute-start | bytes 1179656 | tf_op jit(solution)/shard_map/ppermute | solution.py:64
  8.8 1.0 copy-start.1
  8.9 1.0 copy-start.2
  28.6 1.0 copy-start.6
  28.6 1.0 copy-start.11
  29.5 1.8 %copy-start.7 = (bf16[1,1,256,128]{3,2,1,0:T(8,128)(2,1)S(1)}, bf16[1,1,256,128]{3,2,1,0:T(8,128)(2,1)}, u32[]{:S(2)}) copy-start(bf16[1,1,256,128]{3,2,1,0:T(8,128)(2,1)} %slice.173) | copy-start | bytes 196612
  29.5 1.8 %copy-start.8 = (bf16[1,1,256,128]{3,2,1,0:T(8,128)(2,1)S(1)}, bf16[1,1,256,128]{3,2,1,0:T(8,128)(2,1)}, u32[]{:S(2)}) copy-start(bf16[1,1,256,128]{3,2,1,0:T(8,128)(2,1)} %slice.153) | copy-start | bytes 196612
  32.2 0.9 copy-start.10
  33.2 1.0 copy-start.5
  37.3 17.2 %all-to-all-start = ((bf16[8,288,128]{2,1,0:T(8,128)(2,1)}), bf16[8,288,128]{2,1,0:T(8,128)(2,1)S(1)}, u32[]{:S(2)}, u32[]{:S(2)}) async-start(bf16[8,288,128]{2,1,0:T(8,128)(2,1)} %bitcast.31), calls=%async_computation | async-start | bytes 1179648 | tf_op jit(solution)/shard_map/all_to_all | solution.py:89
  56.3 17.9 %collective-permute-start.4 = (f32[289,128]{1,0:T(8,128)S(1)}, f32[289,128]{1,0:T(8,128)}, u32[]{:S(2)}, u32[]{:S(2)}) collective-permute-start(f32[289,128]{1,0:T(8,128)S(1)} %concatenate.72), channel_id=1, source_target_pairs={{0,128},{8,136},{16,144},{24,152},{32,160},{40,168},{48,176},{56,1... | collective-permute-start | bytes 443912 | tf_op jit(solution)/shard_map/cond/branch_4_fun/ppermute | solution.py:14
  77.8 14.0 %all-to-all-start.1 = ((bf16[8,288,128]{2,1,0:T(8,128)(2,1)}), bf16[8,288,128]{2,1,0:T(8,128)(2,1)S(1)}, u32[]{:S(2)}, u32[]{:S(2)}) async-start(bf16[8,288,128]{2,1,0:T(8,128)(2,1)} %broadcast_in_dim.32), calls=%async_computation.1 | async-start | bytes 1179648 | tf_op jit(solution)/shard_map/all_to_all | solution.py:95
  82.1 0.7 copy-start.3
  93.6 0.9 copy-start.9
  94.5 1.0 copy-start.4
  94.5 1.1 copy-start.12
  97.9 14.0 %all-to-all-start.2 = ((bf16[8,288,128]{2,1,0:T(8,128)(2,1)}), bf16[8,288,128]{2,1,0:T(8,128)(2,1)S(1)}, u32[]{:S(2)}, u32[]{:S(2)}) async-start(bf16[8,288,128]{2,1,0:T(8,128)(2,1)} %bitcast.57), calls=%async_computation.2 | async-start | bytes 1179648 | tf_op jit(solution)/shard_map/all_to_all | solution.py:89
  113.0 29.3 %collective-permute-start.11 = (f32[289,128]{1,0:T(8,128)S(1)}, f32[289,128]{1,0:T(8,128)}, u32[]{:S(2)}, u32[]{:S(2)}) collective-permute-start(f32[289,128]{1,0:T(8,128)S(1)} %concatenate.79), channel_id=1, source_target_pairs={{0,256},{8,264},{16,272},{24,280},{32,288},{40,296},{48,304},{56,3... | collective-permute-start | bytes 443912 | tf_op jit(solution)/shard_map/cond/branch_5_fun/ppermute | solution.py:14
  144.3 22.7 %all-to-all-start.3 = ((f32[8,288,128]{2,1,0:T(8,128)}), f32[8,288,128]{2,1,0:T(8,128)S(1)}, u32[]{:S(2)}, u32[]{:S(2)}) async-start(f32[8,288,128]{2,1,0:T(8,128)} %broadcast_in_dim.33), calls=%async_computation.3 | async-start | bytes 2359296 | tf_op jit(solution)/shard_map/all_to_all | solution.py:95

commit v4 on v3

--- a/solution.py
+++ b/solution.py
@@ -56,9 +56,9 @@
 
 def halo_rows(images, out_grads):
     tiles = lax.axis_size("tile")
-    own_rows = images.shape[3]
-    for_below = jnp.concatenate([images[:, 0], out_grads[:, 0, :, own_rows - 1 :]], axis=2)
-    for_above = jnp.concatenate([images[:, 0], out_grads[:, 0, :, :1]], axis=2)
+    own_rows = images.shape[2]
+    for_below = jnp.concatenate([images[0], out_grads[0, :, own_rows - 1 :]], axis=1)
+    for_above = jnp.concatenate([images[0], out_grads[0, :, :1]], axis=1)
     down = [(i, i + 1) for i in range(tiles - 1)]
     up = [(i + 1, i) for i in range(tiles - 1)]
     return lax.ppermute(for_below, "tile", down), lax.ppermute(for_above, "tile", up)
@@ -110,7 +110,6 @@
     state_rows = full_state.size // (tiles * channels)
     sum_state = full_state.reshape(tiles, state_rows, channels)[tile]
     weight = push_weight[0]
-    above, below = halo_rows(images, out_grads)
     own_rows = images.shape[3]
     for step_num in range(images.shape[0]):
         peer_level = (step_index[0] + step_num) % levels
@@ -120,15 +119,22 @@
             weights = gathered((sum_state / weight).astype(jnp.bfloat16), tiles).reshape(
                 kernel_shape
             )
+        if step_num == 0:
+            above, below = halo_rows(images[0], out_grads[0])
+        else:
+            above, below = halo_rows(*step_inputs)
         x_ext = jnp.concatenate(
-            [above[step_num][:, :own_rows], images[step_num, 0], below[step_num][:, :own_rows]],
-            axis=1,
+            [above[:, :own_rows], images[step_num, 0], below[:, :own_rows]], axis=1
         )
         g_ext = jnp.concatenate(
-            [above[step_num][:, own_rows:], out_grads[step_num, 0], below[step_num][:, own_rows:]],
-            axis=1,
+            [above[:, own_rows:], out_grads[step_num, 0], below[:, own_rows:]], axis=1
         )
-        grads_chunk = scattered_sum(local_grads(x_ext, g_ext, weights, first, last), tiles)
+        grads = local_grads(x_ext, g_ext, weights, first, last)
+        if step_num + 1 < images.shape[0]:
+            grads, *step_inputs = lax.optimization_barrier(
+                (grads, images[step_num + 1], out_grads[step_num + 1])
+            )
+        grads_chunk = scattered_sum(grads, tiles)
         sum_state = sum_state - learn_rate * grads_chunk
         got = pushed(with_weight(sum_state, weight), peer_level)
         sum_state = 0.5 * (sum_state + got[:state_rows])

time: 170 us -> 162 us (0.953)
  the two profiles are of different devices: /device:TPU:2 before, /device:TPU:224 now
where the time goes in v4:
time: 162 us; the launch traced here: 161 us
  waiting for transfers between devices  75.5 us (47%)
  starting transfers between devices  46.8 us (29%)
  local copies, waits for them, and re-layouts  18.9 us (12%)
  matrix products  8.52 us (5%)
  other arithmetic  6.19 us (4%)
  between operations  5.01 us (3%)
    all_to_all x2, waiting for transfers between devices, gathered(): return lax.all_to_all(spread, 'tile', 0, 0, tiled=True)  26.6 us
    ppermute x2, waiting for transfers between devices, passed_along(): lax.ppermute(shard, axis, [(i, (i + by) % devices) for i in range(devices)])  22.9 us
    all_to_all x2, waiting for transfers between devices, scattered_sum(): got = lax.all_to_all(chunks, 'tile', 0, 0, tiled=True)  19.5 us
    ppermute x2, starting transfers between devices, passed_along(): lax.ppermute(shard, axis, [(i, (i + by) % devices) for i in range(devices)])  15.7 us
    all_to_all x2, starting transfers between devices, scattered_sum(): got = lax.all_to_all(chunks, 'tile', 0, 0, tiled=True)  11.3 us
    ppermute x2, starting transfers between devices, halo_rows(): lax.ppermute(for_below, 'tile', down)  9.88 us
    all_to_all x2, starting transfers between devices, gathered(): return lax.all_to_all(spread, 'tile', 0, 0, tiled=True)  7.28 us
    unnamed x37, local copies, waits for them, and re-layouts  6.7 us
  transfers between devices with their start and end apart: 10, of which 8 were waited for; matrix products, arithmetic and copies ran while one was open for 3% of the time, Pallas kernels for 0%

profile of v4, /device:TPU:224, one launch (start us, length us, event | category | flops | bytes accessed | tf_op | source)
XLA Modules:
  0.0 161.0 jit_solution(9484770962557213058)
XLA Ops:
  0.6 1.1 slice_bitcast_fusion.1
  1.8 1.1 slice_bitcast_fusion.4
  2.9 4.9 %collective-permute-start.12 = (bf16[1,3,256,128]{3,2,1,0:T(8,128)(2,1)S(1)}, bf16[1,3,256,128]{3,2,1,0:T(8,128)(2,1)S(1)}, u32[]{:S(2)}, u32[]{:S(2)}) collective-permute-start(bf16[1,3,256,128]{3,2,1,0:T(8,128)(2,1)S(1)} %get-tuple-element.95), channel_id=1, source_target_pairs={{0,1},{1,2},{2,3},{3,4},{4,5},{5,6},{6,7},{8,9},{9,10},{10,11},{11... | collective-permute-start | bytes 589832 | tf_op jit(solution)/shard_map/ppermute | solution.py:64
  7.8 1.3 collective-permute-start.13
  11.0 0.9 collective-permute-done.12
  12.6 5.5 %collective-permute-done.13 = bf16[1,3,256,128]{3,2,1,0:T(8,128)(2,1)S(1)} collective-permute-done((bf16[1,3,256,128]{3,2,1,0:T(8,128)(2,1)S(1)}, bf16[1,3,256,128]{3,2,1,0:T(8,128)(2,1)S(1)}, u32[]{:S(2)}, u32[]{:S(2)}) %collective-permute-start.13) | collective-permute-done | bytes 196640 | tf_op jit(solution)/shard_map/ppermute | solution.py:64
  20.4 1.7 %fusion.106 = (bf16[4,8,33,128]{3,1,2,0:T(8,128)(2,1)S(1)}, f32[4,8,33,128]{3,1,2,0:T(8,128)}) fusion(pred[4]{0:T(512)(128)(4,1)S(1)} %and_or_fusion, pred[8,33]{0,1:T(8,128)(4,1)S(1)} %copy-done.10, bf16[3,3,128,128]{3,2,1,0:T(8,128)(2,1)S(1)} %bitcast.151, bf16[6,1,7,2,128]{4,2,3,0,1:T(8,128)(2,1)S(1)} %slice.148, bf16[6,1,8,33,128]{4,2,3,0,1:T(8,128)(2,1)S(1)} %copy.22), kind=kOutput, calls=%fused_computation.117 | convolution fusion | flops 313933824 | bytes 1533196 | tf_op jit(solution)/shard_map/conv_general_dilated | solution.py:25
  24.9 2.3 %convolution_multiply_fusion.1 = bf16[3,3,128,128,1]{3,2,1,4,0:T(8,128)(2,1)S(1)} fusion(bf16[6,8,33,128,1]{3,1,4,2,0:T(8,128)(2,1)S(1)} %get-tuple-element.106, bf16[6,8,33,128,1]{3,1,4,2,0:T(8,128)(2,1)S(1)} %copy.17, bf16[6,8,33,128,1]{3,1,4,2,0:T(8,128)(2,1)S(1)} %get-tuple-element.105, bf16[3,3,128,128]{3,2,1,0:T(8,128)(2,1)S(1)} %bitcast.150, ...), kind=kOutput, calls=%fused_computation.1 | convolution fusion | flops 317042688 | bytes 2361608 | tf_op jit(solution)/shard_map/transpose | solution.py:54
  28.1 4.9 %collective-permute-start.14 = (bf16[1,3,256,128]{3,2,1,0:T(8,128)(2,1)S(1)}, bf16[1,3,256,128]{3,2,1,0:T(8,128)(2,1)S(1)}, u32[]{:S(2)}, u32[]{:S(2)}) collective-permute-start(bf16[1,3,256,128]{3,2,1,0:T(8,128)(2,1)S(1)} %get-tuple-element.91), channel_id=1, source_target_pairs={{0,1},{1,2},{2,3},{3,4},{4,5},{5,6},{6,7},{8,9},{9,10},{10,11},{11... | collective-permute-start | bytes 589832 | tf_op jit(solution)/shard_map/ppermute | solution.py:64
  33.1 1.3 collective-permute-start.15
  34.4 7.8 %all-to-all-start = ((bf16[8,288,128]{2,1,0:T(8,128)(2,1)}), bf16[8,288,128]{2,1,0:T(8,128)(2,1)S(1)}, u32[]{:S(2)}, u32[]{:S(2)}) async-start(bf16[8,288,128]{2,1,0:T(8,128)(2,1)} %bitcast.29), calls=%async_computation | async-start | bytes 1179648 | tf_op jit(solution)/shard_map/all_to_all | solution.py:89
  44.5 8.5 %all-to-all-done = bf16[8,288,128]{2,1,0:T(8,128)(2,1)S(1)} async-done(((bf16[8,288,128]{2,1,0:T(8,128)(2,1)}), bf16[8,288,128]{2,1,0:T(8,128)(2,1)S(1)}, u32[]{:S(2)}, u32[]{:S(2)}) %all-to-all-start) | async-done | bytes 589856 | tf_op jit(solution)/shard_map/all_to_all | solution.py:89
  53.1 0.9 bitcast_subtract_fusion
  54.0 17.9 %conditional.2 = (f32[289,128]{1,0:T(8,128)}) conditional(s32[]{:T(128)} %clamp.6, (f32[288,128]{1,0:T(8,128)S(1)}, f32[]{:T(128)}) %tuple.47, (f32[288,128]{1,0:T(8,128)S(1)}, f32[]{:T(128)}) %tuple.47, (f32[288,128]{1,0:T(8,128)S(1)}, f32[]{:T(128)}) %tuple.47, (f32[288,128]{1,0:T(8,128)S(1)}, f32[]{:T(128)}) %tuple.47, ...), branch_computations={%region_1.2_spmd, %region_2.3_spmd, %region_3.4_spmd, %region_4.5_... | conditional | bytes 887348 | solution.py:20
  54.7 6.4 %collective-permute-start.4 = (f32[289,128]{1,0:T(8,128)S(1)}, f32[289,128]{1,0:T(8,128)}, u32[]{:S(2)}, u32[]{:S(2)}) collective-permute-start(f32[289,128]{1,0:T(8,128)S(1)} %concatenate.80), channel_id=1, source_target_pairs={{0,128},{8,136},{16,144},{24,152},{32,160},{40,168},{48,176},{56,1... | collective-permute-start | bytes 443912 | tf_op jit(solution)/shard_map/cond/branch_4_fun/ppermute | solution.py:14
  61.1 10.8 %collective-permute-done.4 = f32[289,128]{1,0:T(8,128)} collective-permute-done((f32[289,128]{1,0:T(8,128)S(1)}, f32[289,128]{1,0:T(8,128)}, u32[]{:S(2)}, u32[]{:S(2)}) %collective-permute-start.4) | collective-permute-done | bytes 148000 | tf_op jit(solution)/shard_map/cond/branch_4_fun/ppermute | solution.py:14
  72.0 1.2 slice.165
  75.7 3.7 %all-to-all-start.1 = ((bf16[8,288,128]{2,1,0:T(8,128)(2,1)}), bf16[8,288,128]{2,1,0:T(8,128)(2,1)S(1)}, u32[]{:S(2)}, u32[]{:S(2)}) async-start(bf16[8,288,128]{2,1,0:T(8,128)(2,1)} %broadcast_in_dim.32), calls=%async_computation.1 | async-start | bytes 1179648 | tf_op jit(solution)/shard_map/all_to_all | solution.py:95
  81.6 9.8 %all-to-all-done.1 = bf16[8,288,128]{2,1,0:T(8,128)(2,1)S(1)} async-done(((bf16[8,288,128]{2,1,0:T(8,128)(2,1)}), bf16[8,288,128]{2,1,0:T(8,128)(2,1)S(1)}, u32[]{:S(2)}, u32[]{:S(2)}) %all-to-all-start.1) | async-done | bytes 589856 | tf_op jit(solution)/shard_map/all_to_all | solution.py:95
  91.4 1.7 %fusion.107 = (bf16[4,8,33,128]{3,1,2,0:T(8,128)(2,1)S(1)}, f32[4,8,33,128]{3,1,2,0:T(8,128)}) fusion(pred[4]{0:T(512)(128)(4,1)S(1)} %and_or_fusion, pred[8,33]{0,1:T(8,128)(4,1)S(1)} %copy-done.10, bf16[3,3,128,128]{3,2,1,0:T(8,128)(2,1)S(1)} %bitcast.157, bf16[6,1,7,2,128]{4,2,3,0,1:T(8,128)(2,1)S(1)} %slice.167, bf16[6,1,8,33,128]{4,2,3,0,1:T(8,128)(2,1)S(1)} %copy.36), kind=kOutput, calls=%fused_computation.118 | convolution fusion | flops 313933824 | bytes 1533196 | tf_op jit(solution)/shard_map/conv_general_dilated | solution.py:25
  95.2 1.4 fusion.12
  97.4 3.5 %all-to-all-start.2 = ((bf16[8,288,128]{2,1,0:T(8,128)(2,1)}), bf16[8,288,128]{2,1,0:T(8,128)(2,1)S(1)}, u32[]{:S(2)}, u32[]{:S(2)}) async-start(bf16[8,288,128]{2,1,0:T(8,128)(2,1)} %bitcast.56), calls=%async_computation.2 | async-start | bytes 1179648 | tf_op jit(solution)/shard_map/all_to_all | solution.py:89
  101.0 11.0 %all-to-all-done.2 = bf16[8,288,128]{2,1,0:T(8,128)(2,1)S(1)} async-done(((bf16[8,288,128]{2,1,0:T(8,128)(2,1)}), bf16[8,288,128]{2,1,0:T(8,128)(2,1)S(1)}, u32[]{:S(2)}, u32[]{:S(2)}) %all-to-all-start.2) | async-done | bytes 589856 | tf_op jit(solution)/shard_map/all_to_all | solution.py:89
  112.1 1.0 multiply_subtract_fusion
  113.1 21.5 %conditional.3 = (f32[289,128]{1,0:T(8,128)}) conditional(s32[]{:T(128)} %clamp.7, (f32[288,128]{1,0:T(8,128)S(1)}, f32[]{:T(128)}) %tuple.48, (f32[288,128]{1,0:T(8,128)S(1)}, f32[]{:T(128)}) %tuple.48, (f32[288,128]{1,0:T(8,128)S(1)}, f32[]{:T(128)}) %tuple.48, (f32[288,128]{1,0:T(8,128)S(1)}, f32[]{:T(128)}) %tuple.48, ...), branch_computations={%region_8.9_spmd, %region_9.10_spmd, %region_10.11_spmd, %region_1... | conditional | bytes 887348 | solution.py:20
  113.1 9.3 %collective-permute-start.11 = (f32[289,128]{1,0:T(8,128)S(1)}, f32[289,128]{1,0:T(8,128)}, u32[]{:S(2)}, u32[]{:S(2)}) collective-permute-start(f32[289,128]{1,0:T(8,128)S(1)} %concatenate.87), channel_id=1, source_target_pairs={{0,256},{8,264},{16,272},{24,280},{32,288},{40,296},{48,304},{56,3... | collective-permute-start | bytes 443912 | tf_op jit(solution)/shard_map/cond/branch_5_fun/ppermute | solution.py:14
  122.5 12.1 %collective-permute-done.11 = f32[289,128]{1,0:T(8,128)} collective-permute-done((f32[289,128]{1,0:T(8,128)S(1)}, f32[289,128]{1,0:T(8,128)}, u32[]{:S(2)}, u32[]{:S(2)}) %collective-permute-start.11) | collective-permute-done | bytes 148000 | tf_op jit(solution)/shard_map/cond/branch_5_fun/ppermute | solution.py:14
  135.5 1.1 broadcast_in_dim.33
  136.6 3.6 %all-to-all-start.3 = ((f32[8,288,128]{2,1,0:T(8,128)}), f32[8,288,128]{2,1,0:T(8,128)S(1)}, u32[]{:S(2)}, u32[]{:S(2)}) async-start(f32[8,288,128]{2,1,0:T(8,128)} %broadcast_in_dim.33), calls=%async_computation.3 | async-start | bytes 2359296 | tf_op jit(solution)/shard_map/all_to_all | solution.py:95
  140.2 1.2 slice.175
  142.0 16.9 %all-to-all-done.3 = f32[8,288,128]{2,1,0:T(8,128)S(1)} async-done(((f32[8,288,128]{2,1,0:T(8,128)}), f32[8,288,128]{2,1,0:T(8,128)S(1)}, u32[]{:S(2)}, u32[]{:S(2)}) %all-to-all-start.3) | async-done | bytes 1179680 | tf_op jit(solution)/shard_map/all_to_all | solution.py:95
  158.9 1.0 copy.76
  (109 shorter events, 17.8 us)
Async XLA Ops:
  0.6 9.2 %copy-start = (f32[1,2,1152,128]{3,2,1,0:T(8,128)S(1)}, f32[1,2,1152,128]{3,2,1,0:T(8,128)}, u32[]{:S(2)}) copy-start(f32[1,2,1152,128]{3,2,1,0:T(8,128)} %param.19) | copy-start | bytes 3538948
  2.9 9.1 %collective-permute-start.12 = (bf16[1,3,256,128]{3,2,1,0:T(8,128)(2,1)S(1)}, bf16[1,3,256,128]{3,2,1,0:T(8,128)(2,1)S(1)}, u32[]{:S(2)}, u32[]{:S(2)}) collective-permute-start(bf16[1,3,256,128]{3,2,1,0:T(8,128)(2,1)S(1)} %get-tuple-element.95), channel_id=1, source_target_pairs={{0,1},{1,2},{2,3},{3,4},{4,5},{5,6},{6,7},{8,9},{9,10},{10,11},{11... | collective-permute-start | bytes 589832 | tf_op jit(solution)/shard_map/ppermute | solution.py:64
  7.8 10.3 %collective-permute-start.13 = (bf16[1,3,256,128]{3,2,1,0:T(8,128)(2,1)S(1)}, bf16[1,3,256,128]{3,2,1,0:T(8,128)(2,1)S(1)}, u32[]{:S(2)}, u32[]{:S(2)}) collective-permute-start(bf16[1,3,256,128]{3,2,1,0:T(8,128)(2,1)S(1)} %get-tuple-element.96), channel_id=1, source_target_pairs={{1,0},{2,1},{3,2},{4,3},{5,4},{6,5},{7,6},{9,8},{10,9},{11,10},{12... | collective-permute-start | bytes 589832 | tf_op jit(solution)/shard_map/ppermute | solution.py:64
  12.0 0.7 copy-start.7
  18.2 0.7 copy-start.8
  19.4 1.0 copy-start.4
  19.4 1.0 copy-start.10
  22.1 0.8 slice-start.2
  22.1 0.9 slice-start.3
  23.9 1.0 copy-start.3
  28.1 15.6 %collective-permute-start.14 = (bf16[1,3,256,128]{3,2,1,0:T(8,128)(2,1)S(1)}, bf16[1,3,256,128]{3,2,1,0:T(8,128)(2,1)S(1)}, u32[]{:S(2)}, u32[]{:S(2)}) collective-permute-start(bf16[1,3,256,128]{3,2,1,0:T(8,128)(2,1)S(1)} %get-tuple-element.91), channel_id=1, source_target_pairs={{0,1},{1,2},{2,3},{3,4},{4,5},{5,6},{6,7},{8,9},{9,10},{10,11},{11... | collective-permute-start | bytes 589832 | tf_op jit(solution)/shard_map/ppermute | solution.py:64
  33.1 10.7 %collective-permute-start.15 = (bf16[1,3,256,128]{3,2,1,0:T(8,128)(2,1)S(1)}, bf16[1,3,256,128]{3,2,1,0:T(8,128)(2,1)S(1)}, u32[]{:S(2)}, u32[]{:S(2)}) collective-permute-start(bf16[1,3,256,128]{3,2,1,0:T(8,128)(2,1)S(1)} %get-tuple-element.92), channel_id=1, source_target_pairs={{1,0},{2,1},{3,2},{4,3},{5,4},{6,5},{7,6},{9,8},{10,9},{11,10},{12... | collective-permute-start | bytes 589832 | tf_op jit(solution)/shard_map/ppermute | solution.py:64
  34.4 18.6 %all-to-all-start = ((bf16[8,288,128]{2,1,0:T(8,128)(2,1)}), bf16[8,288,128]{2,1,0:T(8,128)(2,1)S(1)}, u32[]{:S(2)}, u32[]{:S(2)}) async-start(bf16[8,288,128]{2,1,0:T(8,128)(2,1)} %bitcast.29), calls=%async_computation | async-start | bytes 1179648 | tf_op jit(solution)/shard_map/all_to_all | solution.py:89
  43.7 0.7 copy-start.5
  43.7 0.7 copy-start.6
  54.7 17.2 %collective-permute-start.4 = (f32[289,128]{1,0:T(8,128)S(1)}, f32[289,128]{1,0:T(8,128)}, u32[]{:S(2)}, u32[]{:S(2)}) collective-permute-start(f32[289,128]{1,0:T(8,128)S(1)} %concatenate.80), channel_id=1, source_target_pairs={{0,128},{8,136},{16,144},{24,152},{32,160},{40,168},{48,176},{56,1... | collective-permute-start | bytes 443912 | tf_op jit(solution)/shard_map/cond/branch_4_fun/ppermute | solution.py:14
  71.9 7.4 %slice-start = ((bf16[1,3,256,128]{3,2,1,0:T(8,128)(2,1)}), bf16[1,1,256,128]{3,2,1,0:T(8,128)(2,1)S(1)}, s32[]{:S(2)}) async-start(bf16[1,3,256,128]{3,2,1,0:T(8,128)(2,1)} %copy-done.5), calls=%async_computation.4 | async-start | bytes 131072 | tf_op jit(solution)/shard_map/slice | solution.py:130
  71.9 7.4 %slice-start.1 = ((bf16[1,3,256,128]{3,2,1,0:T(8,128)(2,1)}), bf16[1,1,256,128]{3,2,1,0:T(8,128)(2,1)S(1)}, s32[]{:S(2)}) async-start(bf16[1,3,256,128]{3,2,1,0:T(8,128)(2,1)} %copy-done.6), calls=%async_computation.5 | async-start | bytes 131072 | tf_op jit(solution)/shard_map/slice | solution.py:130
  75.7 15.7 %all-to-all-start.1 = ((bf16[8,288,128]{2,1,0:T(8,128)(2,1)}), bf16[8,288,128]{2,1,0:T(8,128)(2,1)S(1)}, u32[]{:S(2)}, u32[]{:S(2)}) async-start(bf16[8,288,128]{2,1,0:T(8,128)(2,1)} %broadcast_in_dim.32), calls=%async_computation.1 | async-start | bytes 1179648 | tf_op jit(solution)/shard_map/all_to_all | solution.py:95
  80.0 0.7 copy-start.1
  93.1 0.9 copy-start.9
  94.0 1.0 copy-start.2
  94.1 1.1 copy-start.11
  97.4 14.6 %all-to-all-start.2 = ((bf16[8,288,128]{2,1,0:T(8,128)(2,1)}), bf16[8,288,128]{2,1,0:T(8,128)(2,1)S(1)}, u32[]{:S(2)}, u32[]{:S(2)}) async-start(bf16[8,288,128]{2,1,0:T(8,128)(2,1)} %bitcast.56), calls=%async_computation.2 | async-start | bytes 1179648 | tf_op jit(solution)/shard_map/all_to_all | solution.py:89
  113.1 21.4 %collective-permute-start.11 = (f32[289,128]{1,0:T(8,128)S(1)}, f32[289,128]{1,0:T(8,128)}, u32[]{:S(2)}, u32[]{:S(2)}) collective-permute-start(f32[289,128]{1,0:T(8,128)S(1)} %concatenate.87), channel_id=1, source_target_pairs={{0,256},{8,264},{16,272},{24,280},{32,288},{40,296},{48,304},{56,3... | collective-permute-start | bytes 443912 | tf_op jit(solution)/shard_map/cond/branch_5_fun/ppermute | solution.py:14
  136.6 22.3 %all-to-all-start.3 = ((f32[8,288,128]{2,1,0:T(8,128)}), f32[8,288,128]{2,1,0:T(8,128)S(1)}, u32[]{:S(2)}, u32[]{:S(2)}) async-start(f32[8,288,128]{2,1,0:T(8,128)} %broadcast_in_dim.33), calls=%async_computation.3 | async-start | bytes 2359296 | tf_op jit(solution)/shard_map/all_to_all | solution.py:95

commit v5 on v4

--- a/solution.py
+++ b/solution.py
@@ -96,7 +96,17 @@
 
 
 def with_weight(chunk, weight):
-    return jnp.concatenate([chunk, jnp.broadcast_to(weight, (1, chunk.shape[-1]))], axis=0)
+    high = weight.astype(jnp.bfloat16)
+    rest = weight - high.astype(jnp.float32)
+    middle = rest.astype(jnp.bfloat16)
+    low = (rest - middle.astype(jnp.float32)).astype(jnp.bfloat16)
+    parts = jnp.zeros((1, chunk.shape[-1]), jnp.bfloat16).at[0, :3].set(jnp.stack([high, middle, low]))
+    return jnp.concatenate([chunk.astype(jnp.bfloat16), parts], axis=0)
+
+
+def weight_of(row):
+    parts = row.astype(jnp.float32)
+    return parts[0] + (parts[1] + parts[2])
 
 
 def shards(images, out_grads, numerators, push_weight, step_index):
@@ -137,8 +147,8 @@
         grads_chunk = scattered_sum(grads, tiles)
         sum_state = sum_state - learn_rate * grads_chunk
         got = pushed(with_weight(sum_state, weight), peer_level)
-        sum_state = 0.5 * (sum_state + got[:state_rows])
-        weight = 0.5 * (weight + got[state_rows, 0])
+        sum_state = 0.5 * (sum_state + got[:state_rows].astype(jnp.float32))
+        weight = 0.5 * (weight + weight_of(got[state_rows]))
     new_state = gathered(sum_state, tiles).reshape(kernel_shape)
     return (new_state[None], jnp.reshape(weight, (1,)))
 

time: 162 us -> 140 us (0.86)
  the two profiles are of different devices: /device:TPU:224 before, /device:TPU:2 now
where the time goes in v5:
time: 140 us; the launch traced here: 138 us
  waiting for transfers between devices  60.2 us (43%)
  starting transfers between devices  35 us (25%)
  local copies, waits for them, and re-layouts  17.1 us (12%)
  other arithmetic  9.79 us (7%)
  matrix products  8.51 us (6%)
  between operations  7.75 us (6%)
    all_to_all x2, waiting for transfers between devices, gathered(): return lax.all_to_all(spread, 'tile', 0, 0, tiled=True)  18.3 us
    all_to_all x2, waiting for transfers between devices, scattered_sum(): got = lax.all_to_all(chunks, 'tile', 0, 0, tiled=True)  17.4 us
    ppermute x2, waiting for transfers between devices, passed_along(): lax.ppermute(shard, axis, [(i, (i + by) % devices) for i in range(devices)])  17.1 us
    all_to_all x2, starting transfers between devices, scattered_sum(): got = lax.all_to_all(chunks, 'tile', 0, 0, tiled=True)  11.3 us
    ppermute x2, starting transfers between devices, halo_rows(): lax.ppermute(for_below, 'tile', down)  8.08 us
    all_to_all x2, starting transfers between devices, gathered(): return lax.all_to_all(spread, 'tile', 0, 0, tiled=True)  7.28 us
    unnamed x37, local copies, waits for them, and re-layouts  6.69 us
    ppermute x2, waiting for transfers between devices, halo_rows(): lax.ppermute(for_above, 'tile', up)  6.42 us
  transfers between devices with their start and end apart: 10, of which 8 were waited for; matrix products, arithmetic and copies ran while one was open for 5% of the time, Pallas kernels for 0%

profile of v5, /device:TPU:2, one launch (start us, length us, event | category | flops | bytes accessed | tf_op | source)
XLA Modules:
  0.0 138.4 jit_solution(6481484383332304608)
XLA Ops:
  0.6 1.1 slice_bitcast_fusion.1
  1.8 1.1 slice_bitcast_fusion.4
  2.9 4.0 %collective-permute-start.12 = (bf16[1,3,256,128]{3,2,1,0:T(8,128)(2,1)S(1)}, bf16[1,3,256,128]{3,2,1,0:T(8,128)(2,1)S(1)}, u32[]{:S(2)}, u32[]{:S(2)}) collective-permute-start(bf16[1,3,256,128]{3,2,1,0:T(8,128)(2,1)S(1)} %get-tuple-element.97), channel_id=1, source_target_pairs={{0,1},{1,2},{2,3},{3,4},{4,5},{5,6},{6,7},{8,9},{9,10},{10,11},{11... | collective-permute-start | bytes 589832 | tf_op jit(solution)/shard_map/ppermute | solution.py:64
  6.9 1.3 collective-permute-start.13
  10.1 0.9 collective-permute-done.12
  11.7 6.4 %collective-permute-done.13 = bf16[1,3,256,128]{3,2,1,0:T(8,128)(2,1)S(1)} collective-permute-done((bf16[1,3,256,128]{3,2,1,0:T(8,128)(2,1)S(1)}, bf16[1,3,256,128]{3,2,1,0:T(8,128)(2,1)S(1)}, u32[]{:S(2)}, u32[]{:S(2)}) %collective-permute-start.13) | collective-permute-done | bytes 196640 | tf_op jit(solution)/shard_map/ppermute | solution.py:64
  20.4 1.7 %fusion.106 = (bf16[4,8,33,128]{3,1,2,0:T(8,128)(2,1)S(1)}, f32[4,8,33,128]{3,1,2,0:T(8,128)}) fusion(pred[4]{0:T(512)(128)(4,1)S(1)} %and_or_fusion, pred[8,33]{0,1:T(8,128)(4,1)S(1)} %copy-done.10, bf16[3,3,128,128]{3,2,1,0:T(8,128)(2,1)S(1)} %bitcast.160, bf16[6,1,7,2,128]{4,2,3,0,1:T(8,128)(2,1)S(1)} %slice.210, bf16[6,1,8,33,128]{4,2,3,0,1:T(8,128)(2,1)S(1)} %copy.22), kind=kOutput, calls=%fused_computation.117 | convolution fusion | flops 313933824 | bytes 1533196 | tf_op jit(solution)/shard_map/conv_general_dilated | solution.py:25
  24.9 2.3 %convolution_multiply_fusion.1 = bf16[3,3,128,128,1]{3,2,1,4,0:T(8,128)(2,1)S(1)} fusion(bf16[6,8,33,128,1]{3,1,4,2,0:T(8,128)(2,1)S(1)} %get-tuple-element.114, bf16[6,8,33,128,1]{3,1,4,2,0:T(8,128)(2,1)S(1)} %copy.17, bf16[6,8,33,128,1]{3,1,4,2,0:T(8,128)(2,1)S(1)} %get-tuple-element.113, bf16[3,3,128,128]{3,2,1,0:T(8,128)(2,1)S(1)} %bitcast.159, ...), kind=kOutput, calls=%fused_computation.1 | convolution fusion | flops 317042688 | bytes 2361608 | tf_op jit(solution)/shard_map/transpose | solution.py:54
  28.1 4.0 %collective-permute-start.14 = (bf16[1,3,256,128]{3,2,1,0:T(8,128)(2,1)S(1)}, bf16[1,3,256,128]{3,2,1,0:T(8,128)(2,1)S(1)}, u32[]{:S(2)}, u32[]{:S(2)}) collective-permute-start(bf16[1,3,256,128]{3,2,1,0:T(8,128)(2,1)S(1)} %get-tuple-element.93), channel_id=1, source_target_pairs={{0,1},{1,2},{2,3},{3,4},{4,5},{5,6},{6,7},{8,9},{9,10},{10,11},{11... | collective-permute-start | bytes 589832 | tf_op jit(solution)/shard_map/ppermute | solution.py:64
  32.2 1.3 collective-permute-start.15
  34.2 7.8 %all-to-all-start = ((bf16[8,288,128]{2,1,0:T(8,128)(2,1)}), bf16[8,288,128]{2,1,0:T(8,128)(2,1)S(1)}, u32[]{:S(2)}, u32[]{:S(2)}) async-start(bf16[8,288,128]{2,1,0:T(8,128)(2,1)} %bitcast.29), calls=%async_computation | async-start | bytes 1179648 | tf_op jit(solution)/shard_map/all_to_all | solution.py:89
  45.1 7.7 %all-to-all-done = bf16[8,288,128]{2,1,0:T(8,128)(2,1)S(1)} async-done(((bf16[8,288,128]{2,1,0:T(8,128)(2,1)}), bf16[8,288,128]{2,1,0:T(8,128)(2,1)S(1)}, u32[]{:S(2)}, u32[]{:S(2)}) %all-to-all-start) | async-done | bytes 589856 | tf_op jit(solution)/shard_map/all_to_all | solution.py:89
  52.9 1.0 fusion.155
  53.9 13.9 %conditional.2 = (bf16[289,128]{1,0:T(8,128)(2,1)}) conditional(s32[]{:T(128)} %clamp.6, bf16[289,128]{1,0:T(8,128)(2,1)S(1)} %fusion.126, bf16[289,128]{1,0:T(8,128)(2,1)S(1)} %fusion.126, bf16[289,128]{1,0:T(8,128)(2,1)S(1)} %fusion.126, bf16[289,128]{1,0:T(8,128)(2,1)S(1)} %fusion.126, ...), branch_computations={%region_2.3_spmd, %region_3.4_spmd, %region_4.5_spmd, %region_5.6_... | conditional | bytes 295984 | solution.py:20
  53.9 3.8 %collective-permute-start.2 = (bf16[289,128]{1,0:T(8,128)(2,1)S(1)}, bf16[289,128]{1,0:T(8,128)(2,1)}, u32[]{:S(2)}, u32[]{:S(2)}) collective-permute-start(bf16[289,128]{1,0:T(8,128)(2,1)S(1)} %param.6), channel_id=1, source_target_pairs={{0,32},{8,40},{16,48},{24,56},{32,64},{40,72},{48,80},{56,88},{64,... | collective-permute-start | bytes 221960 | tf_op jit(solution)/shard_map/cond/branch_2_fun/ppermute | solution.py:14
  57.8 10.0 %collective-permute-done.2 = bf16[289,128]{1,0:T(8,128)(2,1)} collective-permute-done((bf16[289,128]{1,0:T(8,128)(2,1)S(1)}, bf16[289,128]{1,0:T(8,128)(2,1)}, u32[]{:S(2)}, u32[]{:S(2)}) %collective-permute-start.2) | collective-permute-done | bytes 74016 | tf_op jit(solution)/shard_map/cond/branch_2_fun/ppermute | solution.py:14
  71.0 0.9 divide_convert_fusion.1
  72.8 3.7 %all-to-all-start.1 = ((bf16[8,288,128]{2,1,0:T(8,128)(2,1)}), bf16[8,288,128]{2,1,0:T(8,128)(2,1)S(1)}, u32[]{:S(2)}, u32[]{:S(2)}) async-start(bf16[8,288,128]{2,1,0:T(8,128)(2,1)} %broadcast_in_dim.30), calls=%async_computation.1 | async-start | bytes 1179648 | tf_op jit(solution)/shard_map/all_to_all | solution.py:95
  78.8 8.1 %all-to-all-done.1 = bf16[8,288,128]{2,1,0:T(8,128)(2,1)S(1)} async-done(((bf16[8,288,128]{2,1,0:T(8,128)(2,1)}), bf16[8,288,128]{2,1,0:T(8,128)(2,1)S(1)}, u32[]{:S(2)}, u32[]{:S(2)}) %all-to-all-start.1) | async-done | bytes 589856 | tf_op jit(solution)/shard_map/all_to_all | solution.py:95
  86.9 1.7 %fusion.107 = (bf16[4,8,33,128]{3,1,2,0:T(8,128)(2,1)S(1)}, f32[4,8,33,128]{3,1,2,0:T(8,128)}) fusion(pred[4]{0:T(512)(128)(4,1)S(1)} %and_or_fusion, pred[8,33]{0,1:T(8,128)(4,1)S(1)} %copy-done.10, bf16[3,3,128,128]{3,2,1,0:T(8,128)(2,1)S(1)} %bitcast.166, bf16[6,1,7,2,128]{4,2,3,0,1:T(8,128)(2,1)S(1)} %slice.229, bf16[6,1,8,33,128]{4,2,3,0,1:T(8,128)(2,1)S(1)} %copy.36), kind=kOutput, calls=%fused_computation.118 | convolution fusion | flops 313933824 | bytes 1533196 | tf_op jit(solution)/shard_map/conv_general_dilated | solution.py:25
  90.7 1.4 %fusion.12 = bf16[3,3,128,128,1]{3,2,1,4,0:T(8,128)(2,1)S(1)} fusion(bf16[6,8,33,128,1]{3,1,4,2,0:T(8,128)(2,1)S(1)} %fusion.61, bf16[6,8,33,128,1]{3,1,4,2,0:T(8,128)(2,1)S(1)} %copy.31, bf16[6,8,33,128,1]{3,1,4,2,0:T(8,128)(2,1)S(1)} %fusion.57, bf16[3,3,128,128]{3,2,1,0:T(8,128)(2,1)S(1)} %bitcast.161, bf16[4,1,7,2,128]{4,2,3,0,1:T(8,128)(2,1)S(1)} %slice.226, ...), kind=kOutput, calls=%fused_computation.18 | convolution fusion | flops 317042688 | bytes 2368512 | tf_op jit(solution)/shard_map/transpose | solution.py:54
  92.9 3.5 %all-to-all-start.2 = ((bf16[8,288,128]{2,1,0:T(8,128)(2,1)}), bf16[8,288,128]{2,1,0:T(8,128)(2,1)S(1)}, u32[]{:S(2)}, u32[]{:S(2)}) async-start(bf16[8,288,128]{2,1,0:T(8,128)(2,1)} %bitcast.59), calls=%async_computation.2 | async-start | bytes 1179648 | tf_op jit(solution)/shard_map/all_to_all | solution.py:89
  97.3 9.7 %all-to-all-done.2 = bf16[8,288,128]{2,1,0:T(8,128)(2,1)S(1)} async-done(((bf16[8,288,128]{2,1,0:T(8,128)(2,1)}), bf16[8,288,128]{2,1,0:T(8,128)(2,1)S(1)}, u32[]{:S(2)}, u32[]{:S(2)}) %all-to-all-start.2) | async-done | bytes 589856 | tf_op jit(solution)/shard_map/all_to_all | solution.py:89
  107.0 0.9 fusion.154
  108.0 9.0 %conditional.3 = (bf16[289,128]{1,0:T(8,128)(2,1)}) conditional(s32[]{:T(128)} %clamp.7, bf16[289,128]{1,0:T(8,128)(2,1)S(1)} %fusion.127, bf16[289,128]{1,0:T(8,128)(2,1)S(1)} %fusion.127, bf16[289,128]{1,0:T(8,128)(2,1)S(1)} %fusion.127, bf16[289,128]{1,0:T(8,128)(2,1)S(1)} %fusion.127, ...), branch_computations={%region_9.10_spmd, %region_10.11_spmd, %region_11.12_spmd, %region... | conditional | bytes 295984 | solution.py:20
  108.0 1.9 %collective-permute-start.9 = (bf16[289,128]{1,0:T(8,128)(2,1)S(1)}, bf16[289,128]{1,0:T(8,128)(2,1)}, u32[]{:S(2)}, u32[]{:S(2)}) collective-permute-start(bf16[289,128]{1,0:T(8,128)(2,1)S(1)} %param.13), channel_id=1, source_target_pairs={{0,64},{8,72},{16,80},{24,88},{32,96},{40,104},{48,112},{56,120},{... | collective-permute-start | bytes 221960 | tf_op jit(solution)/shard_map/cond/branch_3_fun/ppermute | solution.py:14
  109.9 7.1 %collective-permute-done.9 = bf16[289,128]{1,0:T(8,128)(2,1)} collective-permute-done((bf16[289,128]{1,0:T(8,128)(2,1)S(1)}, bf16[289,128]{1,0:T(8,128)(2,1)}, u32[]{:S(2)}, u32[]{:S(2)}) %collective-permute-start.9) | collective-permute-done | bytes 74016 | tf_op jit(solution)/shard_map/cond/branch_3_fun/ppermute | solution.py:14
  117.0 1.0 add_multiply_fusion
  118.0 1.1 broadcast_in_dim.31
  119.1 3.6 %all-to-all-start.3 = ((f32[8,288,128]{2,1,0:T(8,128)}), f32[8,288,128]{2,1,0:T(8,128)S(1)}, u32[]{:S(2)}, u32[]{:S(2)}) async-start(f32[8,288,128]{2,1,0:T(8,128)} %broadcast_in_dim.31), calls=%async_computation.3 | async-start | bytes 2359296 | tf_op jit(solution)/shard_map/all_to_all | solution.py:95
  126.0 10.3 %all-to-all-done.3 = f32[8,288,128]{2,1,0:T(8,128)S(1)} async-done(((f32[8,288,128]{2,1,0:T(8,128)}), f32[8,288,128]{2,1,0:T(8,128)S(1)}, u32[]{:S(2)}, u32[]{:S(2)}) %all-to-all-start.3) | async-done | bytes 1179680 | tf_op jit(solution)/shard_map/all_to_all | solution.py:95
  136.3 1.0 copy.76
  (114 shorter events, 20.2 us)
Async XLA Ops:
  0.6 8.3 %copy-start = (f32[1,2,1152,128]{3,2,1,0:T(8,128)S(1)}, f32[1,2,1152,128]{3,2,1,0:T(8,128)}, u32[]{:S(2)}) copy-start(f32[1,2,1152,128]{3,2,1,0:T(8,128)} %param.23) | copy-start | bytes 3538948
  2.9 8.2 %collective-permute-start.12 = (bf16[1,3,256,128]{3,2,1,0:T(8,128)(2,1)S(1)}, bf16[1,3,256,128]{3,2,1,0:T(8,128)(2,1)S(1)}, u32[]{:S(2)}, u32[]{:S(2)}) collective-permute-start(bf16[1,3,256,128]{3,2,1,0:T(8,128)(2,1)S(1)} %get-tuple-element.97), channel_id=1, source_target_pairs={{0,1},{1,2},{2,3},{3,4},{4,5},{5,6},{6,7},{8,9},{9,10},{10,11},{11... | collective-permute-start | bytes 589832 | tf_op jit(solution)/shard_map/ppermute | solution.py:64
  6.9 11.2 %collective-permute-start.13 = (bf16[1,3,256,128]{3,2,1,0:T(8,128)(2,1)S(1)}, bf16[1,3,256,128]{3,2,1,0:T(8,128)(2,1)S(1)}, u32[]{:S(2)}, u32[]{:S(2)}) collective-permute-start(bf16[1,3,256,128]{3,2,1,0:T(8,128)(2,1)S(1)} %get-tuple-element.98), channel_id=1, source_target_pairs={{1,0},{2,1},{3,2},{4,3},{5,4},{6,5},{7,6},{9,8},{10,9},{11,10},{12... | collective-permute-start | bytes 589832 | tf_op jit(solution)/shard_map/ppermute | solution.py:64
  11.1 0.7 copy-start.7
  18.2 0.7 copy-start.8
  19.4 1.0 copy-start.4
  19.4 1.0 copy-start.10
  22.1 0.8 slice-start.2
  22.1 0.9 slice-start.3
  23.9 1.0 copy-start.3
  28.1 16.2 %collective-permute-start.14 = (bf16[1,3,256,128]{3,2,1,0:T(8,128)(2,1)S(1)}, bf16[1,3,256,128]{3,2,1,0:T(8,128)(2,1)S(1)}, u32[]{:S(2)}, u32[]{:S(2)}) collective-permute-start(bf16[1,3,256,128]{3,2,1,0:T(8,128)(2,1)S(1)} %get-tuple-element.93), channel_id=1, source_target_pairs={{0,1},{1,2},{2,3},{3,4},{4,5},{5,6},{6,7},{8,9},{9,10},{10,11},{11... | collective-permute-start | bytes 589832 | tf_op jit(solution)/shard_map/ppermute | solution.py:64
  32.2 12.2 %collective-permute-start.15 = (bf16[1,3,256,128]{3,2,1,0:T(8,128)(2,1)S(1)}, bf16[1,3,256,128]{3,2,1,0:T(8,128)(2,1)S(1)}, u32[]{:S(2)}, u32[]{:S(2)}) collective-permute-start(bf16[1,3,256,128]{3,2,1,0:T(8,128)(2,1)S(1)} %get-tuple-element.94), channel_id=1, source_target_pairs={{1,0},{2,1},{3,2},{4,3},{5,4},{6,5},{7,6},{9,8},{10,9},{11,10},{12... | collective-permute-start | bytes 589832 | tf_op jit(solution)/shard_map/ppermute | solution.py:64
  34.2 18.6 %all-to-all-start = ((bf16[8,288,128]{2,1,0:T(8,128)(2,1)}), bf16[8,288,128]{2,1,0:T(8,128)(2,1)S(1)}, u32[]{:S(2)}, u32[]{:S(2)}) async-start(bf16[8,288,128]{2,1,0:T(8,128)(2,1)} %bitcast.29), calls=%async_computation | async-start | bytes 1179648 | tf_op jit(solution)/shard_map/all_to_all | solution.py:89
  44.3 0.7 copy-start.5
  44.4 0.7 copy-start.6
  53.9 22.7 %slice-start = ((bf16[1,3,256,128]{3,2,1,0:T(8,128)(2,1)}), bf16[1,1,256,128]{3,2,1,0:T(8,128)(2,1)S(1)}, s32[]{:S(2)}) async-start(bf16[1,3,256,128]{3,2,1,0:T(8,128)(2,1)} %copy-done.5), calls=%async_computation.4 | async-start | bytes 131072 | tf_op jit(solution)/shard_map/slice | solution.py:140
  53.9 22.7 %slice-start.1 = ((bf16[1,3,256,128]{3,2,1,0:T(8,128)(2,1)}), bf16[1,1,256,128]{3,2,1,0:T(8,128)(2,1)S(1)}, s32[]{:S(2)}) async-start(bf16[1,3,256,128]{3,2,1,0:T(8,128)(2,1)} %copy-done.6), calls=%async_computation.5 | async-start | bytes 131072 | tf_op jit(solution)/shard_map/slice | solution.py:140
  53.9 13.9 %collective-permute-start.2 = (bf16[289,128]{1,0:T(8,128)(2,1)S(1)}, bf16[289,128]{1,0:T(8,128)(2,1)}, u32[]{:S(2)}, u32[]{:S(2)}) collective-permute-start(bf16[289,128]{1,0:T(8,128)(2,1)S(1)} %param.6), channel_id=1, source_target_pairs={{0,32},{8,40},{16,48},{24,56},{32,64},{40,72},{48,80},{56,88},{64,... | collective-permute-start | bytes 221960 | tf_op jit(solution)/shard_map/cond/branch_2_fun/ppermute | solution.py:14
  72.8 14.0 %all-to-all-start.1 = ((bf16[8,288,128]{2,1,0:T(8,128)(2,1)}), bf16[8,288,128]{2,1,0:T(8,128)(2,1)S(1)}, u32[]{:S(2)}, u32[]{:S(2)}) async-start(bf16[8,288,128]{2,1,0:T(8,128)(2,1)} %broadcast_in_dim.30), calls=%async_computation.1 | async-start | bytes 1179648 | tf_op jit(solution)/shard_map/all_to_all | solution.py:95
  77.1 0.7 copy-start.1
  88.6 0.9 copy-start.9
  89.5 1.0 copy-start.2
  89.5 1.1 copy-start.11
  92.9 14.0 %all-to-all-start.2 = ((bf16[8,288,128]{2,1,0:T(8,128)(2,1)}), bf16[8,288,128]{2,1,0:T(8,128)(2,1)S(1)}, u32[]{:S(2)}, u32[]{:S(2)}) async-start(bf16[8,288,128]{2,1,0:T(8,128)(2,1)} %bitcast.59), calls=%async_computation.2 | async-start | bytes 1179648 | tf_op jit(solution)/shard_map/all_to_all | solution.py:89
  108.0 9.0 %collective-permute-start.9 = (bf16[289,128]{1,0:T(8,128)(2,1)S(1)}, bf16[289,128]{1,0:T(8,128)(2,1)}, u32[]{:S(2)}, u32[]{:S(2)}) collective-permute-start(bf16[289,128]{1,0:T(8,128)(2,1)S(1)} %param.13), channel_id=1, source_target_pairs={{0,64},{8,72},{16,80},{24,88},{32,96},{40,104},{48,112},{56,120},{... | collective-permute-start | bytes 221960 | tf_op jit(solution)/shard_map/cond/branch_3_fun/ppermute | solution.py:14
  119.1 17.2 %all-to-all-start.3 = ((f32[8,288,128]{2,1,0:T(8,128)}), f32[8,288,128]{2,1,0:T(8,128)S(1)}, u32[]{:S(2)}, u32[]{:S(2)}) async-start(f32[8,288,128]{2,1,0:T(8,128)} %broadcast_in_dim.31), calls=%async_computation.3 | async-start | bytes 2359296 | tf_op jit(solution)/shard_map/all_to_all | solution.py:95

commit v6 on v5

--- a/solution.py
+++ b/solution.py
@@ -149,7 +149,8 @@
         got = pushed(with_weight(sum_state, weight), peer_level)
         sum_state = 0.5 * (sum_state + got[:state_rows].astype(jnp.float32))
         weight = 0.5 * (weight + weight_of(got[state_rows]))
-    new_state = gathered(sum_state, tiles).reshape(kernel_shape)
+    new_state = gathered(sum_state.astype(jnp.bfloat16), tiles).reshape(kernel_shape)
+    new_state = new_state.astype(jnp.float32)
     return (new_state[None], jnp.reshape(weight, (1,)))
 
 

time: 140 us -> 134 us (0.957)
  the two profiles are of different devices: /device:TPU:2 before, /device:TPU:8 now
where the time goes in v6:
time: 134 us; the launch traced here: 133 us
  waiting for transfers between devices  46.7 us (35%)
  starting transfers between devices  43.4 us (32%)
  local copies, waits for them, and re-layouts  15.9 us (12%)
  other arithmetic  10.9 us (8%)
  matrix products  8.51 us (6%)
  between operations  7.67 us (6%)
    ppermute x2, waiting for transfers between devices, passed_along(): lax.ppermute(shard, axis, [(i, (i + by) % devices) for i in range(devices)])  17 us
    all_to_all x2, waiting for transfers between devices, scattered_sum(): got = lax.all_to_all(chunks, 'tile', 0, 0, tiled=True)  13.6 us
    all_to_all x2, waiting for transfers between devices, gathered(): return lax.all_to_all(spread, 'tile', 0, 0, tiled=True)  11.6 us
    all_to_all x2, starting transfers between devices, scattered_sum(): got = lax.all_to_all(chunks, 'tile', 0, 0, tiled=True)  11.6 us
    all_to_all x2, starting transfers between devices, gathered(): return lax.all_to_all(spread, 'tile', 0, 0, tiled=True)  10.9 us
    ppermute x2, starting transfers between devices, halo_rows(): lax.ppermute(for_below, 'tile', down)  9.87 us
    ppermute x2, starting transfers between devices, halo_rows(): lax.ppermute(for_above, 'tile', up)  6.62 us
    unnamed x36, local copies, waits for them, and re-layouts  5.68 us
  transfers between devices with their start and end apart: 10, of which 8 were waited for; matrix products, arithmetic and copies ran while one was open for 6% of the time, Pallas kernels for 0%

profile of v6, /device:TPU:8, one launch (start us, length us, event | category | flops | bytes accessed | tf_op | source)
XLA Modules:
  0.0 133.2 jit_solution(3929589257623460210)
XLA Ops:
  0.6 1.1 slice_bitcast_fusion.1
  1.8 1.1 slice_bitcast_fusion.4
  2.9 4.9 %collective-permute-start.12 = (bf16[1,3,256,128]{3,2,1,0:T(8,128)(2,1)S(1)}, bf16[1,3,256,128]{3,2,1,0:T(8,128)(2,1)S(1)}, u32[]{:S(2)}, u32[]{:S(2)}) collective-permute-start(bf16[1,3,256,128]{3,2,1,0:T(8,128)(2,1)S(1)} %get-tuple-element.97), channel_id=1, source_target_pairs={{0,1},{1,2},{2,3},{3,4},{4,5},{5,6},{6,7},{8,9},{9,10},{10,11},{11... | collective-permute-start | bytes 589832 | tf_op jit(solution)/shard_map/ppermute | solution.py:64
  7.8 3.3 %collective-permute-start.13 = (bf16[1,3,256,128]{3,2,1,0:T(8,128)(2,1)S(1)}, bf16[1,3,256,128]{3,2,1,0:T(8,128)(2,1)S(1)}, u32[]{:S(2)}, u32[]{:S(2)}) collective-permute-start(bf16[1,3,256,128]{3,2,1,0:T(8,128)(2,1)S(1)} %get-tuple-element.98), channel_id=1, source_target_pairs={{1,0},{2,1},{3,2},{4,3},{5,4},{6,5},{7,6},{9,8},{10,9},{11,10},{12... | collective-permute-start | bytes 589832 | tf_op jit(solution)/shard_map/ppermute | solution.py:64
  13.0 1.3 collective-permute-done.12
  15.0 3.2 %collective-permute-done.13 = bf16[1,3,256,128]{3,2,1,0:T(8,128)(2,1)S(1)} collective-permute-done((bf16[1,3,256,128]{3,2,1,0:T(8,128)(2,1)S(1)}, bf16[1,3,256,128]{3,2,1,0:T(8,128)(2,1)S(1)}, u32[]{:S(2)}, u32[]{:S(2)}) %collective-permute-start.13) | collective-permute-done | bytes 196640 | tf_op jit(solution)/shard_map/ppermute | solution.py:64
  20.4 1.7 %fusion.106 = (bf16[4,8,33,128]{3,1,2,0:T(8,128)(2,1)S(1)}, f32[4,8,33,128]{3,1,2,0:T(8,128)}) fusion(pred[4]{0:T(512)(128)(4,1)S(1)} %and_or_fusion, pred[8,33]{0,1:T(8,128)(4,1)S(1)} %copy-done.10, bf16[3,3,128,128]{3,2,1,0:T(8,128)(2,1)S(1)} %bitcast.161, bf16[6,1,7,2,128]{4,2,3,0,1:T(8,128)(2,1)S(1)} %slice.210, bf16[6,1,8,33,128]{4,2,3,0,1:T(8,128)(2,1)S(1)} %copy.22), kind=kOutput, calls=%fused_computation.117 | convolution fusion | flops 313933824 | bytes 1533196 | tf_op jit(solution)/shard_map/conv_general_dilated | solution.py:25
  24.9 2.3 %convolution_multiply_fusion.1 = bf16[3,3,128,128,1]{3,2,1,4,0:T(8,128)(2,1)S(1)} fusion(bf16[6,8,33,128,1]{3,1,4,2,0:T(8,128)(2,1)S(1)} %get-tuple-element.114, bf16[6,8,33,128,1]{3,1,4,2,0:T(8,128)(2,1)S(1)} %copy.17, bf16[6,8,33,128,1]{3,1,4,2,0:T(8,128)(2,1)S(1)} %get-tuple-element.113, bf16[3,3,128,128]{3,2,1,0:T(8,128)(2,1)S(1)} %bitcast.160, ...), kind=kOutput, calls=%fused_computation.1 | convolution fusion | flops 317042688 | bytes 2361608 | tf_op jit(solution)/shard_map/transpose | solution.py:54
  28.1 4.9 %collective-permute-start.14 = (bf16[1,3,256,128]{3,2,1,0:T(8,128)(2,1)S(1)}, bf16[1,3,256,128]{3,2,1,0:T(8,128)(2,1)S(1)}, u32[]{:S(2)}, u32[]{:S(2)}) collective-permute-start(bf16[1,3,256,128]{3,2,1,0:T(8,128)(2,1)S(1)} %get-tuple-element.93), channel_id=1, source_target_pairs={{0,1},{1,2},{2,3},{3,4},{4,5},{5,6},{6,7},{8,9},{9,10},{10,11},{11... | collective-permute-start | bytes 589832 | tf_op jit(solution)/shard_map/ppermute | solution.py:64
  33.1 3.3 %collective-permute-start.15 = (bf16[1,3,256,128]{3,2,1,0:T(8,128)(2,1)S(1)}, bf16[1,3,256,128]{3,2,1,0:T(8,128)(2,1)S(1)}, u32[]{:S(2)}, u32[]{:S(2)}) collective-permute-start(bf16[1,3,256,128]{3,2,1,0:T(8,128)(2,1)S(1)} %get-tuple-element.94), channel_id=1, source_target_pairs={{1,0},{2,1},{3,2},{4,3},{5,4},{6,5},{7,6},{9,8},{10,9},{11,10},{12... | collective-permute-start | bytes 589832 | tf_op jit(solution)/shard_map/ppermute | solution.py:64
  37.1 6.2 %all-to-all-start = ((bf16[8,288,128]{2,1,0:T(8,128)(2,1)}), bf16[8,288,128]{2,1,0:T(8,128)(2,1)S(1)}, u32[]{:S(2)}, u32[]{:S(2)}) async-start(bf16[8,288,128]{2,1,0:T(8,128)(2,1)} %bitcast.29), calls=%async_computation | async-start | bytes 1179648 | tf_op jit(solution)/shard_map/all_to_all | solution.py:89
  46.5 5.8 %all-to-all-done = bf16[8,288,128]{2,1,0:T(8,128)(2,1)S(1)} async-done(((bf16[8,288,128]{2,1,0:T(8,128)(2,1)}), bf16[8,288,128]{2,1,0:T(8,128)(2,1)S(1)}, u32[]{:S(2)}, u32[]{:S(2)}) %all-to-all-start) | async-done | bytes 589856 | tf_op jit(solution)/shard_map/all_to_all | solution.py:89
  52.3 1.0 fusion.155
  53.3 13.9 %conditional.2 = (bf16[289,128]{1,0:T(8,128)(2,1)}) conditional(s32[]{:T(128)} %clamp.6, bf16[289,128]{1,0:T(8,128)(2,1)S(1)} %fusion.126, bf16[289,128]{1,0:T(8,128)(2,1)S(1)} %fusion.126, bf16[289,128]{1,0:T(8,128)(2,1)S(1)} %fusion.126, bf16[289,128]{1,0:T(8,128)(2,1)S(1)} %fusion.126, ...), branch_computations={%region_2.3_spmd, %region_3.4_spmd, %region_4.5_spmd, %region_5.6_... | conditional | bytes 295984 | solution.py:20
  53.3 2.5 %collective-permute-start.1 = (bf16[289,128]{1,0:T(8,128)(2,1)S(1)}, bf16[289,128]{1,0:T(8,128)(2,1)}, u32[]{:S(2)}, u32[]{:S(2)}) collective-permute-start(bf16[289,128]{1,0:T(8,128)(2,1)S(1)} %param.5), channel_id=1, source_target_pairs={{0,16},{8,24},{16,32},{24,40},{32,48},{40,56},{48,64},{56,72},{64,... | collective-permute-start | bytes 221960 | tf_op jit(solution)/shard_map/cond/branch_1_fun/ppermute | solution.py:14
  55.8 11.4 %collective-permute-done.1 = bf16[289,128]{1,0:T(8,128)(2,1)} collective-permute-done((bf16[289,128]{1,0:T(8,128)(2,1)S(1)}, bf16[289,128]{1,0:T(8,128)(2,1)}, u32[]{:S(2)}, u32[]{:S(2)}) %collective-permute-start.1) | collective-permute-done | bytes 74016 | tf_op jit(solution)/shard_map/cond/branch_1_fun/ppermute | solution.py:14
  70.4 0.9 divide_convert_fusion.1
  71.4 0.9 broadcast_in_dim.31
  72.3 5.5 %all-to-all-start.1 = ((bf16[8,288,128]{2,1,0:T(8,128)(2,1)}), bf16[8,288,128]{2,1,0:T(8,128)(2,1)S(1)}, u32[]{:S(2)}, u32[]{:S(2)}) async-start(bf16[8,288,128]{2,1,0:T(8,128)(2,1)} %broadcast_in_dim.31), calls=%async_computation.1 | async-start | bytes 1179648 | tf_op jit(solution)/shard_map/all_to_all | solution.py:95
  79.9 6.4 %all-to-all-done.1 = bf16[8,288,128]{2,1,0:T(8,128)(2,1)S(1)} async-done(((bf16[8,288,128]{2,1,0:T(8,128)(2,1)}), bf16[8,288,128]{2,1,0:T(8,128)(2,1)S(1)}, u32[]{:S(2)}, u32[]{:S(2)}) %all-to-all-start.1) | async-done | bytes 589856 | tf_op jit(solution)/shard_map/all_to_all | solution.py:95
  86.4 1.7 %fusion.107 = (bf16[4,8,33,128]{3,1,2,0:T(8,128)(2,1)S(1)}, f32[4,8,33,128]{3,1,2,0:T(8,128)}) fusion(pred[4]{0:T(512)(128)(4,1)S(1)} %and_or_fusion, pred[8,33]{0,1:T(8,128)(4,1)S(1)} %copy-done.10, bf16[3,3,128,128]{3,2,1,0:T(8,128)(2,1)S(1)} %bitcast.167, bf16[6,1,7,2,128]{4,2,3,0,1:T(8,128)(2,1)S(1)} %slice.229, bf16[6,1,8,33,128]{4,2,3,0,1:T(8,128)(2,1)S(1)} %copy.36), kind=kOutput, calls=%fused_computation.118 | convolution fusion | flops 313933824 | bytes 1533196 | tf_op jit(solution)/shard_map/conv_general_dilated | solution.py:25
  90.1 1.4 %fusion.12 = bf16[3,3,128,128,1]{3,2,1,4,0:T(8,128)(2,1)S(1)} fusion(bf16[6,8,33,128,1]{3,1,4,2,0:T(8,128)(2,1)S(1)} %fusion.61, bf16[6,8,33,128,1]{3,1,4,2,0:T(8,128)(2,1)S(1)} %copy.31, bf16[6,8,33,128,1]{3,1,4,2,0:T(8,128)(2,1)S(1)} %fusion.57, bf16[3,3,128,128]{3,2,1,0:T(8,128)(2,1)S(1)} %bitcast.162, bf16[4,1,7,2,128]{4,2,3,0,1:T(8,128)(2,1)S(1)} %slice.226, ...), kind=kOutput, calls=%fused_computation.18 | convolution fusion | flops 317042688 | bytes 2368512 | tf_op jit(solution)/shard_map/transpose | solution.py:54
  92.4 5.4 %all-to-all-start.2 = ((bf16[8,288,128]{2,1,0:T(8,128)(2,1)}), bf16[8,288,128]{2,1,0:T(8,128)(2,1)S(1)}, u32[]{:S(2)}, u32[]{:S(2)}) async-start(bf16[8,288,128]{2,1,0:T(8,128)(2,1)} %bitcast.59), calls=%async_computation.2 | async-start | bytes 1179648 | tf_op jit(solution)/shard_map/all_to_all | solution.py:89
  98.6 7.9 %all-to-all-done.2 = bf16[8,288,128]{2,1,0:T(8,128)(2,1)S(1)} async-done(((bf16[8,288,128]{2,1,0:T(8,128)(2,1)}), bf16[8,288,128]{2,1,0:T(8,128)(2,1)S(1)}, u32[]{:S(2)}, u32[]{:S(2)}) %all-to-all-start.2) | async-done | bytes 589856 | tf_op jit(solution)/shard_map/all_to_all | solution.py:89
  106.5 0.9 fusion.154
  107.4 7.6 %conditional.3 = (bf16[289,128]{1,0:T(8,128)(2,1)}) conditional(s32[]{:T(128)} %clamp.7, bf16[289,128]{1,0:T(8,128)(2,1)S(1)} %fusion.127, bf16[289,128]{1,0:T(8,128)(2,1)S(1)} %fusion.127, bf16[289,128]{1,0:T(8,128)(2,1)S(1)} %fusion.127, bf16[289,128]{1,0:T(8,128)(2,1)S(1)} %fusion.127, ...), branch_computations={%region_9.10_spmd, %region_10.11_spmd, %region_11.12_spmd, %region... | conditional | bytes 295984 | solution.py:20
  107.5 1.9 %collective-permute-start.8 = (bf16[289,128]{1,0:T(8,128)(2,1)S(1)}, bf16[289,128]{1,0:T(8,128)(2,1)}, u32[]{:S(2)}, u32[]{:S(2)}) collective-permute-start(bf16[289,128]{1,0:T(8,128)(2,1)S(1)} %param.12), channel_id=1, source_target_pairs={{0,32},{8,40},{16,48},{24,56},{32,64},{40,72},{48,80},{56,88},{64,... | collective-permute-start | bytes 221960 | tf_op jit(solution)/shard_map/cond/branch_2_fun/ppermute | solution.py:14
  109.4 5.7 %collective-permute-done.8 = bf16[289,128]{1,0:T(8,128)(2,1)} collective-permute-done((bf16[289,128]{1,0:T(8,128)(2,1)S(1)}, bf16[289,128]{1,0:T(8,128)(2,1)}, u32[]{:S(2)}, u32[]{:S(2)}) %collective-permute-start.8) | collective-permute-done | bytes 74016 | tf_op jit(solution)/shard_map/cond/branch_2_fun/ppermute | solution.py:14
  115.1 1.0 multiply_convert_fusion
  116.9 5.4 %all-to-all-start.3 = ((bf16[8,288,128]{2,1,0:T(8,128)(2,1)}), bf16[8,288,128]{2,1,0:T(8,128)(2,1)S(1)}, u32[]{:S(2)}, u32[]{:S(2)}) async-start(bf16[8,288,128]{2,1,0:T(8,128)(2,1)} %broadcast_in_dim.32), calls=%async_computation.3 | async-start | bytes 1179648 | tf_op jit(solution)/shard_map/all_to_all | solution.py:95
  125.7 5.2 %all-to-all-done.3 = bf16[8,288,128]{2,1,0:T(8,128)(2,1)S(1)} async-done(((bf16[8,288,128]{2,1,0:T(8,128)(2,1)}), bf16[8,288,128]{2,1,0:T(8,128)(2,1)S(1)}, u32[]{:S(2)}, u32[]{:S(2)}) %all-to-all-start.3) | async-done | bytes 589856 | tf_op jit(solution)/shard_map/all_to_all | solution.py:95
  130.9 1.1 convert.13
  (114 shorter events, 20.2 us)
Async XLA Ops:
  0.6 11.2 %copy-start = (f32[1,2,1152,128]{3,2,1,0:T(8,128)S(1)}, f32[1,2,1152,128]{3,2,1,0:T(8,128)}, u32[]{:S(2)}) copy-start(f32[1,2,1152,128]{3,2,1,0:T(8,128)} %param.23) | copy-start | bytes 3538948
  2.9 11.4 %collective-permute-start.12 = (bf16[1,3,256,128]{3,2,1,0:T(8,128)(2,1)S(1)}, bf16[1,3,256,128]{3,2,1,0:T(8,128)(2,1)S(1)}, u32[]{:S(2)}, u32[]{:S(2)}) collective-permute-start(bf16[1,3,256,128]{3,2,1,0:T(8,128)(2,1)S(1)} %get-tuple-element.97), channel_id=1, source_target_pairs={{0,1},{1,2},{2,3},{3,4},{4,5},{5,6},{6,7},{8,9},{9,10},{10,11},{11... | collective-permute-start | bytes 589832 | tf_op jit(solution)/shard_map/ppermute | solution.py:64
  7.8 10.3 %collective-permute-start.13 = (bf16[1,3,256,128]{3,2,1,0:T(8,128)(2,1)S(1)}, bf16[1,3,256,128]{3,2,1,0:T(8,128)(2,1)S(1)}, u32[]{:S(2)}, u32[]{:S(2)}) collective-permute-start(bf16[1,3,256,128]{3,2,1,0:T(8,128)(2,1)S(1)} %get-tuple-element.98), channel_id=1, source_target_pairs={{1,0},{2,1},{3,2},{4,3},{5,4},{6,5},{7,6},{9,8},{10,9},{11,10},{12... | collective-permute-start | bytes 589832 | tf_op jit(solution)/shard_map/ppermute | solution.py:64
  14.3 0.7 copy-start.7
  18.2 0.7 copy-start.8
  19.4 1.0 copy-start.4
  19.4 1.0 copy-start.10
  22.1 0.8 slice-start.2
  22.1 0.9 slice-start.3
  23.9 1.0 copy-start.3
  28.1 17.5 %collective-permute-start.14 = (bf16[1,3,256,128]{3,2,1,0:T(8,128)(2,1)S(1)}, bf16[1,3,256,128]{3,2,1,0:T(8,128)(2,1)S(1)}, u32[]{:S(2)}, u32[]{:S(2)}) collective-permute-start(bf16[1,3,256,128]{3,2,1,0:T(8,128)(2,1)S(1)} %get-tuple-element.93), channel_id=1, source_target_pairs={{0,1},{1,2},{2,3},{3,4},{4,5},{5,6},{6,7},{8,9},{9,10},{10,11},{11... | collective-permute-start | bytes 589832 | tf_op jit(solution)/shard_map/ppermute | solution.py:64
  33.1 12.6 %collective-permute-start.15 = (bf16[1,3,256,128]{3,2,1,0:T(8,128)(2,1)S(1)}, bf16[1,3,256,128]{3,2,1,0:T(8,128)(2,1)S(1)}, u32[]{:S(2)}, u32[]{:S(2)}) collective-permute-start(bf16[1,3,256,128]{3,2,1,0:T(8,128)(2,1)S(1)} %get-tuple-element.94), channel_id=1, source_target_pairs={{1,0},{2,1},{3,2},{4,3},{5,4},{6,5},{7,6},{9,8},{10,9},{11,10},{12... | collective-permute-start | bytes 589832 | tf_op jit(solution)/shard_map/ppermute | solution.py:64
  37.1 15.1 %all-to-all-start = ((bf16[8,288,128]{2,1,0:T(8,128)(2,1)}), bf16[8,288,128]{2,1,0:T(8,128)(2,1)S(1)}, u32[]{:S(2)}, u32[]{:S(2)}) async-start(bf16[8,288,128]{2,1,0:T(8,128)(2,1)} %bitcast.29), calls=%async_computation | async-start | bytes 1179648 | tf_op jit(solution)/shard_map/all_to_all | solution.py:89
  45.7 0.7 copy-start.5
  45.7 0.7 copy-start.6
  53.3 24.5 %slice-start = ((bf16[1,3,256,128]{3,2,1,0:T(8,128)(2,1)}), bf16[1,1,256,128]{3,2,1,0:T(8,128)(2,1)S(1)}, s32[]{:S(2)}) async-start(bf16[1,3,256,128]{3,2,1,0:T(8,128)(2,1)} %copy-done.5), calls=%async_computation.4 | async-start | bytes 131072 | tf_op jit(solution)/shard_map/slice | solution.py:140
  53.3 24.4 %slice-start.1 = ((bf16[1,3,256,128]{3,2,1,0:T(8,128)(2,1)}), bf16[1,1,256,128]{3,2,1,0:T(8,128)(2,1)S(1)}, s32[]{:S(2)}) async-start(bf16[1,3,256,128]{3,2,1,0:T(8,128)(2,1)} %copy-done.6), calls=%async_computation.5 | async-start | bytes 131072 | tf_op jit(solution)/shard_map/slice | solution.py:140
  53.3 13.9 %collective-permute-start.1 = (bf16[289,128]{1,0:T(8,128)(2,1)S(1)}, bf16[289,128]{1,0:T(8,128)(2,1)}, u32[]{:S(2)}, u32[]{:S(2)}) collective-permute-start(bf16[289,128]{1,0:T(8,128)(2,1)S(1)} %param.5), channel_id=1, source_target_pairs={{0,16},{8,24},{16,32},{24,40},{32,48},{40,56},{48,64},{56,72},{64,... | collective-permute-start | bytes 221960 | tf_op jit(solution)/shard_map/cond/branch_1_fun/ppermute | solution.py:14
  72.3 14.1 %all-to-all-start.1 = ((bf16[8,288,128]{2,1,0:T(8,128)(2,1)}), bf16[8,288,128]{2,1,0:T(8,128)(2,1)S(1)}, u32[]{:S(2)}, u32[]{:S(2)}) async-start(bf16[8,288,128]{2,1,0:T(8,128)(2,1)} %broadcast_in_dim.31), calls=%async_computation.1 | async-start | bytes 1179648 | tf_op jit(solution)/shard_map/all_to_all | solution.py:95
  78.3 0.7 copy-start.1
  88.1 0.9 copy-start.9
  89.0 1.0 copy-start.2
  89.0 1.1 copy-start.11
  92.4 14.0 %all-to-all-start.2 = ((bf16[8,288,128]{2,1,0:T(8,128)(2,1)}), bf16[8,288,128]{2,1,0:T(8,128)(2,1)S(1)}, u32[]{:S(2)}, u32[]{:S(2)}) async-start(bf16[8,288,128]{2,1,0:T(8,128)(2,1)} %bitcast.59), calls=%async_computation.2 | async-start | bytes 1179648 | tf_op jit(solution)/shard_map/all_to_all | solution.py:89
  107.5 7.6 %collective-permute-start.8 = (bf16[289,128]{1,0:T(8,128)(2,1)S(1)}, bf16[289,128]{1,0:T(8,128)(2,1)}, u32[]{:S(2)}, u32[]{:S(2)}) collective-permute-start(bf16[289,128]{1,0:T(8,128)(2,1)S(1)} %param.12), channel_id=1, source_target_pairs={{0,32},{8,40},{16,48},{24,56},{32,64},{40,72},{48,80},{56,88},{64,... | collective-permute-start | bytes 221960 | tf_op jit(solution)/shard_map/cond/branch_2_fun/ppermute | solution.py:14
  116.9 14.0 %all-to-all-start.3 = ((bf16[8,288,128]{2,1,0:T(8,128)(2,1)}), bf16[8,288,128]{2,1,0:T(8,128)(2,1)S(1)}, u32[]{:S(2)}, u32[]{:S(2)}) async-start(bf16[8,288,128]{2,1,0:T(8,128)(2,1)} %broadcast_in_dim.32), calls=%async_computation.3 | async-start | bytes 1179648 | tf_op jit(solution)/shard_map/all_to_all | solution.py:95
